TPU v7x, 256 devices: a whole 4x4x8 slice. The times are simulated.
256 devices in a mesh: dp: 32 (over z, x_hi, core), tm: 8 (over y, x_lo).
Axes of the slice: x: 4 (x_hi: 2, x_lo: 2; x = x_hi * 2 + x_lo), y: 4, z: 8, core: 2. Of those that a mesh axis runs over, the one named last changes fastest.
Arguments:
- queries: bfloat16 [32, 3072, 256], P('dp', 'tm'), may hold values from -6 to 6
- key_input: bfloat16 [32, 3072, 256], P('dp', 'tm'), may hold values from -6 to 6
- value_input: bfloat16 [32, 3072, 256], P('dp', 'tm'), may hold values from -6 to 6
- lengths: int32 [32], P('dp'), may hold values from 1536 to 3072, as said below
- projection: bfloat16 [4096, 256], P('dp'), may hold values from -0.09375 to 0.09375
- upstream: bfloat16 [32, 3072, 4096], P('dp', 'tm'), may hold values from -6 to 6
- glu_input: bfloat16 [32, 3072, 4096], P('dp', 'tm'), may hold values from -6 to 6
- kernel: bfloat16 [2048, 31], P('dp'), may hold values from -1 to 1
- norm_gain: bfloat16 [2048], P('dp'), may hold values from 0.5 to 1.5
- conv_upstream: bfloat16 [32, 3072, 2048], P('dp', 'tm'), may hold values from -6 to 6
Outputs:
- grad_queries: bfloat16 [32, 3072, 256], P('dp', 'tm')
- grad_keys: bfloat16 [32, 3072, 256], P('dp', 'tm')
- grad_values: bfloat16 [32, 3072, 256], P('dp', 'tm')
- grad_projection: bfloat16 [4096, 256], P('dp')
- grad_glu: bfloat16 [32, 3072, 4096], P('dp', 'tm')
- grad_kernel: float32 [2048, 31], P('dp')
- grad_gain: float32 [2048], P('dp')
Inputs may be any that keep to these rules, and one draw needn't show every extreme that they name: `lengths`: the valid frames of an utterance are its first ones; one utterance has all 3072 valid and one exactly 1536.
All inputs are finite; a program needn't handle non-finite values.
Results may differ from a plain program's by a relative error of at most 0.02.
Values may be sent and summed in bfloat16 or wider, within the bound.
No kernel may reach another device: no remote copies, remote signals or barrier semaphores. Data moves between devices by JAX's collectives and lax.ppermute only.
A program may use at most 128 MiB of HBM per device.

v0:
```python
import jax
import jax.numpy as jnp
from jax import lax
from jax.sharding import PartitionSpec as P

HEADS = 2
HDIM = 128
CH = 2048
KW = 31
NEG_FILL = -1e30
NORM_EPS = 1e-05


def from_behind(block, axis, distance):
    devices = range(lax.axis_size(axis))
    route = [((i - distance) % len(devices), i) for i in devices]
    return lax.ppermute(block, axis, route)


def extended(cells, sides, width):
    for axis, dim in sides:
        count = lax.axis_size(axis)
        ends = count - 1
        head = lax.slice_in_dim(cells, 0, width, axis=dim)
        tail = lax.slice_in_dim(cells, cells.shape[dim] - width, cells.shape[dim], axis=dim)
        cells = jnp.concatenate(
            [
                lax.ppermute(tail, axis, [(i, (i + 1) % count) for i in range(ends)]),
                cells,
                lax.ppermute(head, axis, [((i + 1) % count, i) for i in range(ends)]),
            ],
            axis=dim,
        )
    return cells


def depthwise(padded, kernel_f, frame_rows):
    mixed = jnp.zeros((frame_rows, kernel_f.shape[0]), jnp.float32)
    for tap in range(kernel_f.shape[1]):
        mixed = mixed + padded[tap : tap + frame_rows].astype(jnp.float32) * kernel_f[:, tap]
    return mixed


def back_depthwise(grad_pad, kernel_f, frame_rows):
    half_width = (kernel_f.shape[1] - 1) // 2
    result = jnp.zeros((frame_rows, kernel_f.shape[0]), jnp.float32)
    for tap in range(kernel_f.shape[1]):
        begin = 2 * half_width - tap
        result = (
            result + grad_pad[begin : begin + frame_rows].astype(jnp.float32) * kernel_f[:, tap]
        )
    return result


def tap_products(grad_low, padded, frame_rows, tap_count):
    grad_f = grad_low.astype(jnp.float32)
    return jnp.stack(
        [
            jnp.sum(grad_f * padded[tap : tap + frame_rows].astype(jnp.float32), axis=0)
            for tap in range(tap_count)
        ],
        axis=1,
    )


def norm_backward(mixed, gain_f, cotangent, frame_live):
    centre = mixed - jnp.mean(mixed, axis=-1, keepdims=True)
    inv_std = lax.rsqrt(jnp.mean(centre * centre, axis=-1, keepdims=True) + NORM_EPS)
    standard = centre * inv_std
    normed = standard * gain_f
    squash = jax.nn.sigmoid(normed)
    grad_normed = (
        cotangent.astype(jnp.float32) * frame_live * (squash + normed * squash * (1.0 - squash))
    )
    gain_term = jnp.sum(grad_normed * standard, axis=0)
    scaled = grad_normed * gain_f
    grad_conv = inv_std * (
        scaled
        - jnp.mean(scaled, axis=-1, keepdims=True)
        - standard * jnp.mean(scaled * standard, axis=-1, keepdims=True)
    )
    return (grad_conv.astype(jnp.bfloat16), gain_term)


def per_device(
    queries,
    key_input,
    value_input,
    lengths,
    projection,
    upstream,
    glu_input,
    kernel,
    norm_gain,
    conv_upstream,
):
    time_count = lax.axis_size("tm")
    time_rank = lax.axis_index("tm")
    frame_rows = queries.shape[1]
    flat_width = queries.shape[2]
    score_scale = HDIM ** (-0.5)
    length = lengths[0]
    full_proj, full_kernel, full_gain = (
        lax.all_gather(projection, "dp", axis=0, tiled=True),
        lax.all_gather(kernel, "dp", axis=0, tiled=True),
        lax.all_gather(norm_gain, "dp", axis=0, tiled=True),
    )
    query_heads = queries[0].reshape(frame_rows, HEADS, HDIM)
    key_heads = key_input[0].reshape(frame_rows, HEADS, HDIM)
    value_heads = value_input[0].reshape(frame_rows, HEADS, HDIM)

    def block_scores(key_block, key_offset):
        scores = (
            jnp.einsum("qhd,khd->hqk", query_heads, key_block, preferred_element_type=jnp.float32)
            * score_scale
        )
        key_live = key_offset + jnp.arange(key_block.shape[0], dtype=jnp.int32) < length
        return jnp.where(key_live[None, None, :], scores, NEG_FILL)

    def absorb(state_now, key_block, value_block, key_offset):
        run_top, run_total, run_acc = state_now
        scores = block_scores(key_block, key_offset)
        new_top = jnp.maximum(run_top, jnp.max(scores, axis=-1))
        factor = jnp.exp(run_top - new_top)
        weights = jnp.exp(scores - new_top[:, :, None])
        run_total = run_total * factor + jnp.sum(weights, axis=-1)
        contrib = jnp.einsum(
            "hqk,khd->qhd",
            weights,
            value_block.astype(jnp.float32),
            precision=lax.Precision.HIGHEST,
        )
        run_acc = run_acc * jnp.transpose(factor)[:, :, None] + contrib
        return (new_top, run_total, run_acc)

    start_state = (
        jnp.full((HEADS, frame_rows), NEG_FILL, jnp.float32),
        jnp.zeros((HEADS, frame_rows), jnp.float32),
        jnp.zeros((frame_rows, HEADS, HDIM), jnp.float32),
    )

    def forward_step(step, loop_state):
        key_block, value_block, inner = loop_state
        source = (time_rank - step) % time_count
        inner = absorb(inner, key_block, value_block, source * frame_rows)
        key_block, value_block = from_behind((key_block, value_block), "tm", 1)
        return (key_block, value_block, inner)

    key_block, value_block, inner = lax.fori_loop(
        0, time_count - 1, forward_step, (key_heads, value_heads, start_state)
    )
    source = (time_rank - (time_count - 1)) % time_count
    state_now = absorb(inner, key_block, value_block, source * frame_rows)
    run_top, run_total, run_acc = state_now
    log_total = run_top + jnp.log(run_total)
    attended = (run_acc / jnp.transpose(run_total)[:, :, None]).astype(jnp.bfloat16)
    upstream_rows = upstream[0]
    grad_out = jnp.dot(upstream_rows, full_proj, preferred_element_type=jnp.float32).astype(
        jnp.bfloat16
    )
    grad_heads = grad_out.reshape(frame_rows, HEADS, HDIM)
    row_delta = jnp.einsum("qhd,qhd->hq", grad_heads, attended, preferred_element_type=jnp.float32)

    def backward_block(key_block, value_block, key_offset):
        scores = block_scores(key_block, key_offset)
        weights = jnp.exp(scores - log_total[:, :, None])
        weights_low = weights.astype(jnp.bfloat16)
        add_value = jnp.einsum(
            "hqk,qhd->khd", weights_low, grad_heads, preferred_element_type=jnp.float32
        )
        grad_weights = jnp.einsum(
            "qhd,khd->hqk", grad_heads, value_block, preferred_element_type=jnp.float32
        )
        grad_scores = (weights * (grad_weights - row_delta[:, :, None]) * score_scale).astype(
            jnp.bfloat16
        )
        add_query = jnp.einsum(
            "hqk,khd->qhd", grad_scores, key_block, preferred_element_type=jnp.float32
        )
        add_key = jnp.einsum(
            "hqk,qhd->khd", grad_scores, query_heads, preferred_element_type=jnp.float32
        )
        return (add_query, add_key, add_value)

    zero_heads = jnp.zeros((frame_rows, HEADS, HDIM), jnp.float32)

    def pass_grads(key_acc, value_acc):
        return from_behind((key_acc, value_acc), "tm", 1)

    def backward_step(step, loop_state):
        key_block, value_block, key_acc, value_acc, query_acc = loop_state
        source = (time_rank - step) % time_count
        add_query, add_key, add_value = backward_block(key_block, value_block, source * frame_rows)
        key_acc, value_acc = pass_grads(key_acc + add_key, value_acc + add_value)
        key_block, value_block = from_behind((key_block, value_block), "tm", 1)
        return (key_block, value_block, key_acc, value_acc, query_acc + add_query)

    key_block, value_block, key_acc, value_acc, query_acc = lax.fori_loop(
        0,
        time_count - 1,
        backward_step,
        (key_heads, value_heads, zero_heads, zero_heads, zero_heads),
    )
    source = (time_rank - (time_count - 1)) % time_count
    add_query, add_key, add_value = backward_block(key_block, value_block, source * frame_rows)
    key_acc, value_acc = pass_grads(key_acc + add_key, value_acc + add_value)
    query_acc = query_acc + add_query
    grad_queries = query_acc.reshape(1, frame_rows, flat_width).astype(jnp.bfloat16)
    grad_keys = key_acc.reshape(1, frame_rows, flat_width).astype(jnp.bfloat16)
    grad_values = value_acc.reshape(1, frame_rows, flat_width).astype(jnp.bfloat16)
    half_width = (KW - 1) // 2
    frame_ids = time_rank * frame_rows + jnp.arange(frame_rows, dtype=jnp.int32)
    frame_live = (frame_ids < length).astype(jnp.float32)[:, None]
    glu_rows = glu_input[0]
    linear = glu_rows[:, :CH].astype(jnp.float32)
    gate_sig = jax.nn.sigmoid(glu_rows[:, CH:].astype(jnp.float32))
    activ = (linear * gate_sig * frame_live).astype(jnp.bfloat16)
    padded = extended(activ, (("tm", 0),), half_width)
    kernel_f = full_kernel.astype(jnp.float32)
    gain_f = full_gain.astype(jnp.float32)
    mixed = depthwise(padded, kernel_f, frame_rows)
    grad_conv, gain_term = norm_backward(mixed, gain_f, conv_upstream[0], frame_live)
    grad_pad = extended(grad_conv, (("tm", 0),), half_width)
    kernel_term = tap_products(grad_conv, padded, frame_rows, KW)
    grad_activ = back_depthwise(grad_pad, kernel_f, frame_rows) * frame_live
    first_half = grad_activ * gate_sig
    second_half = grad_activ * linear * gate_sig * (1.0 - gate_sig)
    grad_glu = jnp.concatenate([first_half, second_half], axis=-1).astype(jnp.bfloat16)[None]
    attended_flat = attended.reshape(frame_rows, flat_width)
    proj_part = lax.psum_scatter(
        lax.dot_general(
            upstream_rows,
            attended_flat,
            (((0,), (0,)), ((), ())),
            preferred_element_type=jnp.float32,
        ),
        "dp",
        scatter_dimension=0,
        tiled=True,
    )
    kernel_part, gain_part = (
        lax.psum_scatter(kernel_term, "dp", scatter_dimension=0, tiled=True),
        lax.psum_scatter(gain_term, "dp", scatter_dimension=0, tiled=True),
    )
    proj_total, kernel_total, gain_total = lax.psum((proj_part, kernel_part, gain_part), "tm")
    grad_projection = proj_total.astype(jnp.bfloat16)
    return (
        grad_queries,
        grad_keys,
        grad_values,
        grad_projection,
        grad_glu,
        kernel_total,
        gain_total,
    )


def solution(mesh):
    in_specs = (
        P("dp", "tm", None),
        P("dp", "tm", None),
        P("dp", "tm", None),
        P("dp"),
        P("dp", None),
        P("dp", "tm", None),
        P("dp", "tm", None),
        P("dp", None),
        P("dp"),
        P("dp", "tm", None),
    )
    out_specs = (
        P("dp", "tm", None),
        P("dp", "tm", None),
        P("dp", "tm", None),
        P("dp", None),
        P("dp", "tm", None),
        P("dp", None),
        P("dp"),
    )
    return jax.shard_map(
        per_device, mesh=mesh, in_specs=in_specs, out_specs=out_specs, check_vma=False
    )
```

profile of v0, /device:TPU:4, one launch (start us, length us, event | category | flops | bytes accessed | tf_op | source)
XLA Modules:
  0.0 809.6 jit_solution(5044786274540221472)
XLA Ops:
  8.1 3.0 fusion.18
  12.9 3.1 collective-permute-start.8
  17.3 41.1 %all-gather = bf16[32,64,31]{1,2,0:T(8,128)(2,1)S(1)} all-gather(bf16[1,64,31]{1,2,0:T(8,128)(2,1)S(1)} %bitcast.320), channel_id=1, replica_groups=mesh['dp'=32,'tm'=8] {'dp'}, dimensions={0}, use_global_device_ids=true | all-gather | bytes 130944 | tf_op jit(solution)/shard_map/all_gather | solution.py:105
  64.8 64.7 %all-reduce = bf16[2048]{0:T(1024)(128)(2,1)S(1)} all-reduce(bf16[2048]{0:T(1024)(128)(2,1)S(1)} %dynamic-update-slice), channel_id=1, replica_groups=mesh['dp'=32,'tm'=8] {'dp'}, use_global_device_ids=true, to_apply=%add | all-reduce | flops 2048 | bytes 8192
  129.6 43.8 %fusion.190 = (f32[384]{0:T(512)S(1)}, f32[384,2048]{1,0:T(8,128)S(1)}) fusion(f32[2048]{0:T(1024)S(1)} %bitcast.229, bf16[15,2048]{1,0:T(8,128)(2,1)S(1)} %collective-permute-done.9, bf16[384,2048]{1,0:T(8,128)(2,1)} %copy-done.3, f32[2048]{0:T(1024)} %bitcast.231, f32[2048]{0:T(1024)} %bitcast.233, f32[2048]{0:T(1024)} %bitcast.235, f32[2048]{0:T(1024)} %bitcast.237, ...), kind=kLoop, calls=%fused_computation.373 | loop fusion | flops 143916672 | bytes 5096960 | tf_op jit(solution)/shard_map/reduce_sum | solution.py:67
  173.9 3.1 multiply_reduce_fusion
  177.1 12.4 %fusion.98 = (f32[2048]{0:T(1024)}, f32[2048]{0:T(1024)}, f32[2048]{0:T(1024)}, f32[2048]{0:T(1024)}, f32[2048]{0:T(1024)}, /*index=5*/f32[2048]{0:T(1024)}, f32...) fusion(bf16[15,2048]{1,0:T(8,128)(2,1)S(1)} %collective-permute-done.9, ...), kind=kLoop, calls=%fused_computation.234 | loop fusion | flops 49526784 | bytes 9586688 | tf_op jit(solution)/shard_map/reduce_sum | solution.py:59
  189.4 7.3 fusion.97
  196.8 4.7 fusion.82
  201.5 3.6 fusion.81
  205.1 3.5 stack.127
  210.7 9.6 %reduce-scatter.5.cloned.1.call-start = ((), (), s32[]{:S(2)}) async-start(), calls=%async_computation.3 | async-start | bytes 4325376 | tf_op jit(solution)/shard_map/reduce_scatter | solution.py:230
  232.3 88.0 %while.48 = (s32[]{:T(128)}, bf16[384,2,128]{2,0,1:T(8,128)(2,1)}, bf16[384,2,128]{2,0,1:T(8,128)(2,1)}, f32[2,384]{1,0:T(2,128)S(1)}, f32[2,384]{1,0:T(2,128)S(...) while((s32[]{:T(128)}, bf16[384,2,128]{2,0,1:T(8,128)(2,1)}, ...), condition=%wide.region_3.4_spmd.clone, body=%wide.region_0.3_spmd.clone.sunk | while | flops 530552064 | bytes 12043402 | solution.py:149
  233.2 2.6 collective-permute-start
  237.5 2.9 collective-permute-start.1
  242.6 3.2 fusion.255
  249.8 3.0 collective-permute-start.1
  255.1 3.3 fusion.255
  266.7 3.3 fusion.255
  270.0 3.3 collective-permute-done
  280.3 3.3 fusion.255
  291.8 3.3 fusion.255
  303.0 3.3 fusion.255
  306.6 2.8 collective-permute-done.1
  315.2 3.3 fusion.255
  325.9 5.2 collective-permute-start.11
  334.3 67.0 %all-reduce.1 = f32[2048]{0:T(1024)} all-reduce(f32[2048]{0:T(1024)} %get-tuple-element.705), channel_id=4, replica_groups=mesh['dp'=32,'tm'=8] {'dp'}, use_global_device_ids=true, to_apply=%region_48.49.clone | all-reduce | flops 2048 | bytes 16384
  402.9 46.6 %fusion.104 = (bf16[1,384,2048]{2,1,0:T(8,128)(2,1)S(1)}, f32[384,2048]{1,0:T(8,128)S(1)}) fusion(bf16[384,4096]{1,0:T(8,128)(2,1)} %bitcast.213, f32[384]{0:T(512)S(1)} %copy-done.50, f32[2048]{0:T(1024)S(1)} %bitcast.230, bf16[384,2048]{1,0:T(8,128)(2,1)} %copy-done.5, bf16[15,2048]{1,0:T(8,128)(2,1)} %collective-permute-done.11, f32[2048]{0:T(1024)S(1)} %bitcast.232, ...), kind=kLoop, calls=%fused_computation.250 | loop fusion | flops 148635648 | bytes 8242688 | tf_op jit(solution)/shard_map/concatenate | solution.py:228
  454.2 3.0 fusion.174
  459.1 3.2 convolution_bitcast_fusion.4
  465.0 277.5 %while.49 = (s32[]{:T(128)}, bf16[384,2,128]{2,0,1:T(8,128)(2,1)}, bf16[384,2,128]{2,0,1:T(8,128)(2,1)}, f32[384,2,128]{2,0,1:T(8,128)}, f32[384,2,128]{2,0,1:T(...) while((s32[]{:T(128)}, bf16[384,2,128]{2,0,1:T(8,128)(2,1)}, ...), condition=%wide.region_7.8_spmd.clone, body=%wide.region_6.7_spmd.clone.sunk | while | flops 380240640 | bytes 16915696 | solution.py:198
  472.3 2.2 fusion.268
  474.5 2.1 fusion.269
  480.7 2.2 fusion.270
  482.9 18.6 %collective-permute-done.2 = bf16[384,2,128]{2,0,1:T(8,128)(2,1)} collective-permute-done((bf16[384,2,128]{2,0,1:T(8,128)(2,1)}, bf16[384,2,128]{2,0,1:T(8,128)(2,1)}, u32[]{:S(2)}, u32[]{:S(2)}) %collective-permute-start.2) | collective-permute-done | bytes 196640 | tf_op jit(solution)/shard_map/while/body/eval_jaxpr/ppermute | solution.py:17
  501.5 3.1 collective-permute-done.3
  511.9 2.1 fusion.268
  514.1 2.1 fusion.269
  516.2 2.7 collective-permute-start.3
  518.9 2.3 fusion.270
  521.2 29.3 %collective-permute-done.2 = bf16[384,2,128]{2,0,1:T(8,128)(2,1)} collective-permute-done((bf16[384,2,128]{2,0,1:T(8,128)(2,1)}, bf16[384,2,128]{2,0,1:T(8,128)(2,1)}, u32[]{:S(2)}, u32[]{:S(2)}) %collective-permute-start.2) | collective-permute-done | bytes 196640 | tf_op jit(solution)/shard_map/while/body/eval_jaxpr/ppermute | solution.py:17
  550.5 3.5 collective-permute-done.3
  561.3 2.1 fusion.268
  567.5 2.3 fusion.270
  569.8 22.1 %collective-permute-done.2 = bf16[384,2,128]{2,0,1:T(8,128)(2,1)} collective-permute-done((bf16[384,2,128]{2,0,1:T(8,128)(2,1)}, bf16[384,2,128]{2,0,1:T(8,128)(2,1)}, u32[]{:S(2)}, u32[]{:S(2)}) %collective-permute-start.2) | collective-permute-done | bytes 196640 | tf_op jit(solution)/shard_map/while/body/eval_jaxpr/ppermute | solution.py:17
  591.9 2.6 collective-permute-done.3
  601.9 2.1 fusion.268
  606.1 2.3 fusion.270
  608.4 22.2 %collective-permute-done.2 = bf16[384,2,128]{2,0,1:T(8,128)(2,1)} collective-permute-done((bf16[384,2,128]{2,0,1:T(8,128)(2,1)}, bf16[384,2,128]{2,0,1:T(8,128)(2,1)}, u32[]{:S(2)}, u32[]{:S(2)}) %collective-permute-start.2) | collective-permute-done | bytes 196640 | tf_op jit(solution)/shard_map/while/body/eval_jaxpr/ppermute | solution.py:17
  640.1 2.1 fusion.268
  644.4 2.3 fusion.270
  646.7 21.4 %collective-permute-done.2 = bf16[384,2,128]{2,0,1:T(8,128)(2,1)} collective-permute-done((bf16[384,2,128]{2,0,1:T(8,128)(2,1)}, bf16[384,2,128]{2,0,1:T(8,128)(2,1)}, u32[]{:S(2)}, u32[]{:S(2)}) %collective-permute-start.2) | collective-permute-done | bytes 196640 | tf_op jit(solution)/shard_map/while/body/eval_jaxpr/ppermute | solution.py:17
  677.5 2.1 fusion.268
  681.8 2.3 fusion.270
  684.1 20.5 %collective-permute-done.2 = bf16[384,2,128]{2,0,1:T(8,128)(2,1)} collective-permute-done((bf16[384,2,128]{2,0,1:T(8,128)(2,1)}, bf16[384,2,128]{2,0,1:T(8,128)(2,1)}, u32[]{:S(2)}, u32[]{:S(2)}) %collective-permute-start.2) | collective-permute-done | bytes 196640 | tf_op jit(solution)/shard_map/while/body/eval_jaxpr/ppermute | solution.py:17
  714.1 2.1 fusion.268
  716.2 2.1 fusion.269
  718.4 2.3 fusion.270
  720.7 19.7 %collective-permute-done.2 = bf16[384,2,128]{2,0,1:T(8,128)(2,1)} collective-permute-done((bf16[384,2,128]{2,0,1:T(8,128)(2,1)}, bf16[384,2,128]{2,0,1:T(8,128)(2,1)}, u32[]{:S(2)}, u32[]{:S(2)}) %collective-permute-start.2) | collective-permute-done | bytes 196640 | tf_op jit(solution)/shard_map/while/body/eval_jaxpr/ppermute | solution.py:17
  742.5 2.4 convolution_multiply_fusion.2
  744.9 2.6 copy.127
  749.5 2.6 fusion.171
  754.1 2.2 fusion.170
  766.4 35.7 %all-reduce.4 = (bf16[128,256]{0,1:T(8,128)(2,1)S(1)}, f32[64,31]{0,1:T(8,128)}, f32[64]{0:T(128)}) all-reduce(f32[128,256]{0,1:T(8,128)} %reduce-scatter.5.cloned.1.call-done, f32[64,31]{0,1:T(8,128)S(1)} %copy-done.42, f32[64]{0:T(128)} %dynamic-slice.2), channel_id=1, replica_groups=mesh['dp'=32,'tm'=8] {'tm'}, use_global_device_ids=true, to_apply=%region_9.10 | all-reduce | flops 34816 | bytes 212992 | tf_op jit(solution)/shard_map/psum | solution.py:245
  (368 shorter events, 180.7 us)
Async XLA Ops:
  7.2 447.0 %copy-start = (bf16[1,384,4096]{2,1,0:T(8,128)(2,1)S(1)}, bf16[1,384,4096]{2,1,0:T(8,128)(2,1)}, u32[]{:S(2)}) copy-start(bf16[1,384,4096]{2,1,0:T(8,128)(2,1)} %param.19) | copy-start | bytes 9437188
  7.2 445.5 %reduce-scatter.7.cloned.1.call-start = ((), (), s32[]{:S(2)}) async-start(), calls=%async_computation.4 | async-start | bytes 1081344
  12.9 116.7 %collective-permute-start.8 = (bf16[15,2048]{1,0:T(8,128)(2,1)}, bf16[15,2048]{1,0:T(8,128)(2,1)S(1)}, u32[]{:S(2)}, u32[]{:S(2)}) collective-permute-start(bf16[15,2048]{1,0:T(8,128)(2,1)} %get-tuple-element.798), channel_id=1, source_target_pairs={{0,1},{1,2},{2,3},{3,4},{4,5},{5,6},{6,7},{8,9},{9,10},{10,11},{11... | collective-permute-start | bytes 184328 | tf_op jit(solution)/shard_map/ppermute | solution.py:28
  16.0 113.6 %collective-permute-start.9 = (bf16[15,2048]{1,0:T(8,128)(2,1)}, bf16[15,2048]{1,0:T(8,128)(2,1)S(1)}, u32[]{:S(2)}, u32[]{:S(2)}) collective-permute-start(bf16[15,2048]{1,0:T(8,128)(2,1)} %get-tuple-element.799), channel_id=1, source_target_pairs={{1,0},{2,1},{3,2},{4,3},{5,4},{6,5},{7,6},{9,8},{10,9},{11,10},{12... | collective-permute-start | bytes 184328 | tf_op jit(solution)/shard_map/ppermute | solution.py:30
  61.2 112.7 %copy-start.16 = (f32[2048,1]{0,1:T(1,128)}, f32[2048,1]{0,1:T(1,128)S(1)}, u32[]{:S(2)}) copy-start(f32[2048,1]{0,1:T(1,128)S(1)} %get-tuple-element.800) | copy-start | bytes 24580
  61.2 112.7 %copy-start.18 = (f32[2048,1]{0,1:T(1,128)}, f32[2048,1]{0,1:T(1,128)S(1)}, u32[]{:S(2)}) copy-start(f32[2048,1]{0,1:T(1,128)S(1)} %get-tuple-element.801) | copy-start | bytes 24580
  209.9 244.2 %all-gather.3.cloned.1.call-start = ((), (), s32[]{:S(2)}) async-start(), calls=%async_computation.2 | async-start | bytes 2162688 | tf_op jit(solution)/shard_map/all_gather | solution.py:104
  210.7 555.7 %reduce-scatter.5.cloned.1.call-start = ((), (), s32[]{:S(2)}) async-start(), calls=%async_computation.3 | async-start | bytes 4325376 | tf_op jit(solution)/shard_map/reduce_scatter | solution.py:230
  233.2 12.6 %collective-permute-start = (bf16[384,2,128]{2,0,1:T(8,128)(2,1)S(1)}, bf16[384,2,128]{2,0,1:T(8,128)(2,1)}, u32[]{:S(2)}, u32[]{:S(2)}) collective-permute-start(bf16[384,2,128]{2,0,1:T(8,128)(2,1)S(1)} %copy.173), channel_id=1, source_target_pairs={{7,0},{0,1},{1,2},{2,3},{3,4},{4,5},{5,6},{6,7},{15,8},{8,9},{9,10... | collective-permute-start | bytes 589832 | tf_op jit(solution)/shard_map/while/body/eval_jaxpr/ppermute | solution.py:17
  237.5 9.7 %collective-permute-start.1 = (bf16[384,2,128]{2,0,1:T(8,128)(2,1)}, bf16[384,2,128]{2,0,1:T(8,128)(2,1)}, u32[]{:S(2)}, u32[]{:S(2)}) collective-permute-start(bf16[384,2,128]{2,0,1:T(8,128)(2,1)} %copy.174), channel_id=1, source_target_pairs={{7,0},{0,1},{1,2},{2,3},{3,4},{4,5},{5,6},{6,7},{15,8},{8,9},{9,10... | collective-permute-start | bytes 589832 | tf_op jit(solution)/shard_map/while/body/eval_jaxpr/ppermute | solution.py:17
  248.1 10.3 %collective-permute-start = (bf16[384,2,128]{2,0,1:T(8,128)(2,1)S(1)}, bf16[384,2,128]{2,0,1:T(8,128)(2,1)}, u32[]{:S(2)}, u32[]{:S(2)}) collective-permute-start(bf16[384,2,128]{2,0,1:T(8,128)(2,1)S(1)} %copy.173), channel_id=1, source_target_pairs={{7,0},{0,1},{1,2},{2,3},{3,4},{4,5},{5,6},{6,7},{15,8},{8,9},{9,10... | collective-permute-start | bytes 589832 | tf_op jit(solution)/shard_map/while/body/eval_jaxpr/ppermute | solution.py:17
  249.8 10.6 %collective-permute-start.1 = (bf16[384,2,128]{2,0,1:T(8,128)(2,1)}, bf16[384,2,128]{2,0,1:T(8,128)(2,1)}, u32[]{:S(2)}, u32[]{:S(2)}) collective-permute-start(bf16[384,2,128]{2,0,1:T(8,128)(2,1)} %copy.174), channel_id=1, source_target_pairs={{7,0},{0,1},{1,2},{2,3},{3,4},{4,5},{5,6},{6,7},{15,8},{8,9},{9,10... | collective-permute-start | bytes 589832 | tf_op jit(solution)/shard_map/while/body/eval_jaxpr/ppermute | solution.py:17
  261.3 12.0 %collective-permute-start = (bf16[384,2,128]{2,0,1:T(8,128)(2,1)S(1)}, bf16[384,2,128]{2,0,1:T(8,128)(2,1)}, u32[]{:S(2)}, u32[]{:S(2)}) collective-permute-start(bf16[384,2,128]{2,0,1:T(8,128)(2,1)S(1)} %copy.173), channel_id=1, source_target_pairs={{7,0},{0,1},{1,2},{2,3},{3,4},{4,5},{5,6},{6,7},{15,8},{8,9},{9,10... | collective-permute-start | bytes 589832 | tf_op jit(solution)/shard_map/while/body/eval_jaxpr/ppermute | solution.py:17
  262.9 12.5 %collective-permute-start.1 = (bf16[384,2,128]{2,0,1:T(8,128)(2,1)}, bf16[384,2,128]{2,0,1:T(8,128)(2,1)}, u32[]{:S(2)}, u32[]{:S(2)}) collective-permute-start(bf16[384,2,128]{2,0,1:T(8,128)(2,1)} %copy.174), channel_id=1, source_target_pairs={{7,0},{0,1},{1,2},{2,3},{3,4},{4,5},{5,6},{6,7},{15,8},{8,9},{9,10... | collective-permute-start | bytes 589832 | tf_op jit(solution)/shard_map/while/body/eval_jaxpr/ppermute | solution.py:17
  276.3 8.4 %collective-permute-start = (bf16[384,2,128]{2,0,1:T(8,128)(2,1)S(1)}, bf16[384,2,128]{2,0,1:T(8,128)(2,1)}, u32[]{:S(2)}, u32[]{:S(2)}) collective-permute-start(bf16[384,2,128]{2,0,1:T(8,128)(2,1)S(1)} %copy.173), channel_id=1, source_target_pairs={{7,0},{0,1},{1,2},{2,3},{3,4},{4,5},{5,6},{6,7},{15,8},{8,9},{9,10... | collective-permute-start | bytes 589832 | tf_op jit(solution)/shard_map/while/body/eval_jaxpr/ppermute | solution.py:17
  277.9 8.9 %collective-permute-start.1 = (bf16[384,2,128]{2,0,1:T(8,128)(2,1)}, bf16[384,2,128]{2,0,1:T(8,128)(2,1)}, u32[]{:S(2)}, u32[]{:S(2)}) collective-permute-start(bf16[384,2,128]{2,0,1:T(8,128)(2,1)} %copy.174), channel_id=1, source_target_pairs={{7,0},{0,1},{1,2},{2,3},{3,4},{4,5},{5,6},{6,7},{15,8},{8,9},{9,10... | collective-permute-start | bytes 589832 | tf_op jit(solution)/shard_map/while/body/eval_jaxpr/ppermute | solution.py:17
  287.8 7.9 collective-permute-start
  289.4 8.4 %collective-permute-start.1 = (bf16[384,2,128]{2,0,1:T(8,128)(2,1)}, bf16[384,2,128]{2,0,1:T(8,128)(2,1)}, u32[]{:S(2)}, u32[]{:S(2)}) collective-permute-start(bf16[384,2,128]{2,0,1:T(8,128)(2,1)} %copy.174), channel_id=1, source_target_pairs={{7,0},{0,1},{1,2},{2,3},{3,4},{4,5},{5,6},{6,7},{15,8},{8,9},{9,10... | collective-permute-start | bytes 589832 | tf_op jit(solution)/shard_map/while/body/eval_jaxpr/ppermute | solution.py:17
  298.7 7.9 collective-permute-start
  300.3 9.1 %collective-permute-start.1 = (bf16[384,2,128]{2,0,1:T(8,128)(2,1)}, bf16[384,2,128]{2,0,1:T(8,128)(2,1)}, u32[]{:S(2)}, u32[]{:S(2)}) collective-permute-start(bf16[384,2,128]{2,0,1:T(8,128)(2,1)} %copy.174), channel_id=1, source_target_pairs={{7,0},{0,1},{1,2},{2,3},{3,4},{4,5},{5,6},{6,7},{15,8},{8,9},{9,10... | collective-permute-start | bytes 589832 | tf_op jit(solution)/shard_map/while/body/eval_jaxpr/ppermute | solution.py:17
  310.3 8.2 %collective-permute-start = (bf16[384,2,128]{2,0,1:T(8,128)(2,1)S(1)}, bf16[384,2,128]{2,0,1:T(8,128)(2,1)}, u32[]{:S(2)}, u32[]{:S(2)}) collective-permute-start(bf16[384,2,128]{2,0,1:T(8,128)(2,1)S(1)} %copy.173), channel_id=1, source_target_pairs={{7,0},{0,1},{1,2},{2,3},{3,4},{4,5},{5,6},{6,7},{15,8},{8,9},{9,10... | collective-permute-start | bytes 589832 | tf_op jit(solution)/shard_map/while/body/eval_jaxpr/ppermute | solution.py:17
  311.9 8.4 %collective-permute-start.1 = (bf16[384,2,128]{2,0,1:T(8,128)(2,1)}, bf16[384,2,128]{2,0,1:T(8,128)(2,1)}, u32[]{:S(2)}, u32[]{:S(2)}) collective-permute-start(bf16[384,2,128]{2,0,1:T(8,128)(2,1)} %copy.174), channel_id=1, source_target_pairs={{7,0},{0,1},{1,2},{2,3},{3,4},{4,5},{5,6},{6,7},{15,8},{8,9},{9,10... | collective-permute-start | bytes 589832 | tf_op jit(solution)/shard_map/while/body/eval_jaxpr/ppermute | solution.py:17
  320.3 82.4 %copy-start.22 = (f32[2048,1]{0,1:T(1,128)S(1)}, f32[2048,1]{0,1:T(1,128)}, u32[]{:S(2)}) copy-start(f32[2048,1]{0,1:T(1,128)} %get-tuple-element.804) | copy-start | bytes 24580
  320.3 82.4 %copy-start.23 = (f32[2048,1]{0,1:T(1,128)S(1)}, f32[2048,1]{0,1:T(1,128)}, u32[]{:S(2)}) copy-start(f32[2048,1]{0,1:T(1,128)} %get-tuple-element.805) | copy-start | bytes 24580
  320.3 82.4 %copy-start.24 = (f32[2048,1]{0,1:T(1,128)S(1)}, f32[2048,1]{0,1:T(1,128)}, u32[]{:S(2)}) copy-start(f32[2048,1]{0,1:T(1,128)} %get-tuple-element.806) | copy-start | bytes 24580
  320.3 82.4 %copy-start.25 = (f32[2048,1]{0,1:T(1,128)S(1)}, f32[2048,1]{0,1:T(1,128)}, u32[]{:S(2)}) copy-start(f32[2048,1]{0,1:T(1,128)} %get-tuple-element.807) | copy-start | bytes 24580
  320.3 82.4 %copy-start.26 = (f32[2048,1]{0,1:T(1,128)S(1)}, f32[2048,1]{0,1:T(1,128)}, u32[]{:S(2)}) copy-start(f32[2048,1]{0,1:T(1,128)} %get-tuple-element.808) | copy-start | bytes 24580
  320.3 82.4 %copy-start.27 = (f32[2048,1]{0,1:T(1,128)S(1)}, f32[2048,1]{0,1:T(1,128)}, u32[]{:S(2)}) copy-start(f32[2048,1]{0,1:T(1,128)} %get-tuple-element.809) | copy-start | bytes 24580
  320.3 82.4 %copy-start.28 = (f32[2048,1]{0,1:T(1,128)S(1)}, f32[2048,1]{0,1:T(1,128)}, u32[]{:S(2)}) copy-start(f32[2048,1]{0,1:T(1,128)} %get-tuple-element.810) | copy-start | bytes 24580
  320.4 82.4 %copy-start.29 = (f32[2048,1]{0,1:T(1,128)S(1)}, f32[2048,1]{0,1:T(1,128)}, u32[]{:S(2)}) copy-start(f32[2048,1]{0,1:T(1,128)} %get-tuple-element.811) | copy-start | bytes 24580
  320.4 82.4 %copy-start.30 = (f32[2048,1]{0,1:T(1,128)S(1)}, f32[2048,1]{0,1:T(1,128)}, u32[]{:S(2)}) copy-start(f32[2048,1]{0,1:T(1,128)} %get-tuple-element.812) | copy-start | bytes 24580
  320.4 82.4 %copy-start.31 = (f32[2048,1]{0,1:T(1,128)S(1)}, f32[2048,1]{0,1:T(1,128)}, u32[]{:S(2)}) copy-start(f32[2048,1]{0,1:T(1,128)} %get-tuple-element.813) | copy-start | bytes 24580
  324.7 78.0 %collective-permute-start.10 = (bf16[15,2048]{1,0:T(8,128)(2,1)}, bf16[15,2048]{1,0:T(8,128)(2,1)}, u32[]{:S(2)}, u32[]{:S(2)}) collective-permute-start(bf16[15,2048]{1,0:T(8,128)(2,1)} %get-tuple-element.796), channel_id=1, source_target_pairs={{1,0},{2,1},{3,2},{4,3},{5,4},{6,5},{7,6},{9,8},{10,9},{11,10},{12... | collective-permute-start | bytes 184328 | tf_op jit(solution)/shard_map/ppermute | solution.py:30
  325.9 76.7 %collective-permute-start.11 = (bf16[15,2048]{1,0:T(8,128)(2,1)}, bf16[15,2048]{1,0:T(8,128)(2,1)}, u32[]{:S(2)}, u32[]{:S(2)}) collective-permute-start(bf16[15,2048]{1,0:T(8,128)(2,1)} %get-tuple-element.797), channel_id=1, source_target_pairs={{0,1},{1,2},{2,3},{3,4},{4,5},{5,6},{6,7},{8,9},{9,10},{10,11},{11... | collective-permute-start | bytes 184328 | tf_op jit(solution)/shard_map/ppermute | solution.py:28
  474.5 30.1 %collective-permute-start.4 = (f32[384,2,128]{2,0,1:T(8,128)}, f32[384,2,128]{2,0,1:T(8,128)}, u32[]{:S(2)}, u32[]{:S(2)}) collective-permute-start(f32[384,2,128]{2,0,1:T(8,128)} %fusion.268), channel_id=1, source_target_pairs={{7,0},{0,1},{1,2},{2,3},{3,4},{4,5},{5,6},{6,7},{15,8},{8,9},{9,10... | collective-permute-start | bytes 1179656 | tf_op jit(solution)/shard_map/while/body/eval_jaxpr/ppermute | solution.py:17
  476.6 28.0 %collective-permute-start.5 = (f32[384,2,128]{2,0,1:T(8,128)}, f32[384,2,128]{2,0,1:T(8,128)}, u32[]{:S(2)}, u32[]{:S(2)}) collective-permute-start(f32[384,2,128]{2,0,1:T(8,128)} %fusion.269), channel_id=1, source_target_pairs={{7,0},{0,1},{1,2},{2,3},{3,4},{4,5},{5,6},{6,7},{15,8},{8,9},{9,10... | collective-permute-start | bytes 1179656 | tf_op jit(solution)/shard_map/while/body/eval_jaxpr/ppermute | solution.py:17
  477.0 24.5 %collective-permute-start.2 = (bf16[384,2,128]{2,0,1:T(8,128)(2,1)}, bf16[384,2,128]{2,0,1:T(8,128)(2,1)}, u32[]{:S(2)}, u32[]{:S(2)}) collective-permute-start(bf16[384,2,128]{2,0,1:T(8,128)(2,1)} %copy.191), channel_id=1, source_target_pairs={{7,0},{0,1},{1,2},{2,3},{3,4},{4,5},{5,6},{6,7},{15,8},{8,9},{9,10... | collective-permute-start | bytes 589832 | tf_op jit(solution)/shard_map/while/body/eval_jaxpr/ppermute | solution.py:17
  479.0 25.6 %collective-permute-start.3 = (bf16[384,2,128]{2,0,1:T(8,128)(2,1)}, bf16[384,2,128]{2,0,1:T(8,128)(2,1)}, u32[]{:S(2)}, u32[]{:S(2)}) collective-permute-start(bf16[384,2,128]{2,0,1:T(8,128)(2,1)} %copy.192), channel_id=1, source_target_pairs={{7,0},{0,1},{1,2},{2,3},{3,4},{4,5},{5,6},{6,7},{15,8},{8,9},{9,10... | collective-permute-start | bytes 589832 | tf_op jit(solution)/shard_map/while/body/eval_jaxpr/ppermute | solution.py:17
  514.1 39.9 %collective-permute-start.4 = (f32[384,2,128]{2,0,1:T(8,128)}, f32[384,2,128]{2,0,1:T(8,128)}, u32[]{:S(2)}, u32[]{:S(2)}) collective-permute-start(f32[384,2,128]{2,0,1:T(8,128)} %fusion.268), channel_id=1, source_target_pairs={{7,0},{0,1},{1,2},{2,3},{3,4},{4,5},{5,6},{6,7},{15,8},{8,9},{9,10... | collective-permute-start | bytes 1179656 | tf_op jit(solution)/shard_map/while/body/eval_jaxpr/ppermute | solution.py:17
  516.2 37.8 %collective-permute-start.5 = (f32[384,2,128]{2,0,1:T(8,128)}, f32[384,2,128]{2,0,1:T(8,128)}, u32[]{:S(2)}, u32[]{:S(2)}) collective-permute-start(f32[384,2,128]{2,0,1:T(8,128)} %fusion.269), channel_id=1, source_target_pairs={{7,0},{0,1},{1,2},{2,3},{3,4},{4,5},{5,6},{6,7},{15,8},{8,9},{9,10... | collective-permute-start | bytes 1179656 | tf_op jit(solution)/shard_map/while/body/eval_jaxpr/ppermute | solution.py:17
  516.2 34.3 %collective-permute-start.2 = (bf16[384,2,128]{2,0,1:T(8,128)(2,1)}, bf16[384,2,128]{2,0,1:T(8,128)(2,1)}, u32[]{:S(2)}, u32[]{:S(2)}) collective-permute-start(bf16[384,2,128]{2,0,1:T(8,128)(2,1)} %copy.191), channel_id=1, source_target_pairs={{7,0},{0,1},{1,2},{2,3},{3,4},{4,5},{5,6},{6,7},{15,8},{8,9},{9,10... | collective-permute-start | bytes 589832 | tf_op jit(solution)/shard_map/while/body/eval_jaxpr/ppermute | solution.py:17
  516.2 37.8 %collective-permute-start.3 = (bf16[384,2,128]{2,0,1:T(8,128)(2,1)}, bf16[384,2,128]{2,0,1:T(8,128)(2,1)}, u32[]{:S(2)}, u32[]{:S(2)}) collective-permute-start(bf16[384,2,128]{2,0,1:T(8,128)(2,1)} %copy.192), channel_id=1, source_target_pairs={{7,0},{0,1},{1,2},{2,3},{3,4},{4,5},{5,6},{6,7},{15,8},{8,9},{9,10... | collective-permute-start | bytes 589832 | tf_op jit(solution)/shard_map/while/body/eval_jaxpr/ppermute | solution.py:17
  563.5 31.1 %collective-permute-start.4 = (f32[384,2,128]{2,0,1:T(8,128)}, f32[384,2,128]{2,0,1:T(8,128)}, u32[]{:S(2)}, u32[]{:S(2)}) collective-permute-start(f32[384,2,128]{2,0,1:T(8,128)} %fusion.268), channel_id=1, source_target_pairs={{7,0},{0,1},{1,2},{2,3},{3,4},{4,5},{5,6},{6,7},{15,8},{8,9},{9,10... | collective-permute-start | bytes 1179656 | tf_op jit(solution)/shard_map/while/body/eval_jaxpr/ppermute | solution.py:17
  565.6 28.9 %collective-permute-start.5 = (f32[384,2,128]{2,0,1:T(8,128)}, f32[384,2,128]{2,0,1:T(8,128)}, u32[]{:S(2)}, u32[]{:S(2)}) collective-permute-start(f32[384,2,128]{2,0,1:T(8,128)} %fusion.269), channel_id=1, source_target_pairs={{7,0},{0,1},{1,2},{2,3},{3,4},{4,5},{5,6},{6,7},{15,8},{8,9},{9,10... | collective-permute-start | bytes 1179656 | tf_op jit(solution)/shard_map/while/body/eval_jaxpr/ppermute | solution.py:17
  565.6 26.3 %collective-permute-start.2 = (bf16[384,2,128]{2,0,1:T(8,128)(2,1)}, bf16[384,2,128]{2,0,1:T(8,128)(2,1)}, u32[]{:S(2)}, u32[]{:S(2)}) collective-permute-start(bf16[384,2,128]{2,0,1:T(8,128)(2,1)} %copy.191), channel_id=1, source_target_pairs={{7,0},{0,1},{1,2},{2,3},{3,4},{4,5},{5,6},{6,7},{15,8},{8,9},{9,10... | collective-permute-start | bytes 589832 | tf_op jit(solution)/shard_map/while/body/eval_jaxpr/ppermute | solution.py:17
  565.6 28.9 %collective-permute-start.3 = (bf16[384,2,128]{2,0,1:T(8,128)(2,1)}, bf16[384,2,128]{2,0,1:T(8,128)(2,1)}, u32[]{:S(2)}, u32[]{:S(2)}) collective-permute-start(bf16[384,2,128]{2,0,1:T(8,128)(2,1)} %copy.192), channel_id=1, source_target_pairs={{7,0},{0,1},{1,2},{2,3},{3,4},{4,5},{5,6},{6,7},{15,8},{8,9},{9,10... | collective-permute-start | bytes 589832 | tf_op jit(solution)/shard_map/while/body/eval_jaxpr/ppermute | solution.py:17
  604.0 28.8 %collective-permute-start.4 = (f32[384,2,128]{2,0,1:T(8,128)}, f32[384,2,128]{2,0,1:T(8,128)}, u32[]{:S(2)}, u32[]{:S(2)}) collective-permute-start(f32[384,2,128]{2,0,1:T(8,128)} %fusion.268), channel_id=1, source_target_pairs={{7,0},{0,1},{1,2},{2,3},{3,4},{4,5},{5,6},{6,7},{15,8},{8,9},{9,10... | collective-permute-start | bytes 1179656 | tf_op jit(solution)/shard_map/while/body/eval_jaxpr/ppermute | solution.py:17
  606.1 26.7 %collective-permute-start.5 = (f32[384,2,128]{2,0,1:T(8,128)}, f32[384,2,128]{2,0,1:T(8,128)}, u32[]{:S(2)}, u32[]{:S(2)}) collective-permute-start(f32[384,2,128]{2,0,1:T(8,128)} %fusion.269), channel_id=1, source_target_pairs={{7,0},{0,1},{1,2},{2,3},{3,4},{4,5},{5,6},{6,7},{15,8},{8,9},{9,10... | collective-permute-start | bytes 1179656 | tf_op jit(solution)/shard_map/while/body/eval_jaxpr/ppermute | solution.py:17
  606.1 24.6 %collective-permute-start.2 = (bf16[384,2,128]{2,0,1:T(8,128)(2,1)}, bf16[384,2,128]{2,0,1:T(8,128)(2,1)}, u32[]{:S(2)}, u32[]{:S(2)}) collective-permute-start(bf16[384,2,128]{2,0,1:T(8,128)(2,1)} %copy.191), channel_id=1, source_target_pairs={{7,0},{0,1},{1,2},{2,3},{3,4},{4,5},{5,6},{6,7},{15,8},{8,9},{9,10... | collective-permute-start | bytes 589832 | tf_op jit(solution)/shard_map/while/body/eval_jaxpr/ppermute | solution.py:17
  606.1 26.7 %collective-permute-start.3 = (bf16[384,2,128]{2,0,1:T(8,128)(2,1)}, bf16[384,2,128]{2,0,1:T(8,128)(2,1)}, u32[]{:S(2)}, u32[]{:S(2)}) collective-permute-start(bf16[384,2,128]{2,0,1:T(8,128)(2,1)} %copy.192), channel_id=1, source_target_pairs={{7,0},{0,1},{1,2},{2,3},{3,4},{4,5},{5,6},{6,7},{15,8},{8,9},{9,10... | collective-permute-start | bytes 589832 | tf_op jit(solution)/shard_map/while/body/eval_jaxpr/ppermute | solution.py:17
  642.3 27.9 %collective-permute-start.4 = (f32[384,2,128]{2,0,1:T(8,128)}, f32[384,2,128]{2,0,1:T(8,128)}, u32[]{:S(2)}, u32[]{:S(2)}) collective-permute-start(f32[384,2,128]{2,0,1:T(8,128)} %fusion.268), channel_id=1, source_target_pairs={{7,0},{0,1},{1,2},{2,3},{3,4},{4,5},{5,6},{6,7},{15,8},{8,9},{9,10... | collective-permute-start | bytes 1179656 | tf_op jit(solution)/shard_map/while/body/eval_jaxpr/ppermute | solution.py:17
  644.4 25.8 %collective-permute-start.5 = (f32[384,2,128]{2,0,1:T(8,128)}, f32[384,2,128]{2,0,1:T(8,128)}, u32[]{:S(2)}, u32[]{:S(2)}) collective-permute-start(f32[384,2,128]{2,0,1:T(8,128)} %fusion.269), channel_id=1, source_target_pairs={{7,0},{0,1},{1,2},{2,3},{3,4},{4,5},{5,6},{6,7},{15,8},{8,9},{9,10... | collective-permute-start | bytes 1179656 | tf_op jit(solution)/shard_map/while/body/eval_jaxpr/ppermute | solution.py:17
  644.4 23.7 %collective-permute-start.2 = (bf16[384,2,128]{2,0,1:T(8,128)(2,1)}, bf16[384,2,128]{2,0,1:T(8,128)(2,1)}, u32[]{:S(2)}, u32[]{:S(2)}) collective-permute-start(bf16[384,2,128]{2,0,1:T(8,128)(2,1)} %copy.191), channel_id=1, source_target_pairs={{7,0},{0,1},{1,2},{2,3},{3,4},{4,5},{5,6},{6,7},{15,8},{8,9},{9,10... | collective-permute-start | bytes 589832 | tf_op jit(solution)/shard_map/while/body/eval_jaxpr/ppermute | solution.py:17
  644.4 25.8 %collective-permute-start.3 = (bf16[384,2,128]{2,0,1:T(8,128)(2,1)}, bf16[384,2,128]{2,0,1:T(8,128)(2,1)}, u32[]{:S(2)}, u32[]{:S(2)}) collective-permute-start(bf16[384,2,128]{2,0,1:T(8,128)(2,1)} %copy.192), channel_id=1, source_target_pairs={{7,0},{0,1},{1,2},{2,3},{3,4},{4,5},{5,6},{6,7},{15,8},{8,9},{9,10... | collective-permute-start | bytes 589832 | tf_op jit(solution)/shard_map/while/body/eval_jaxpr/ppermute | solution.py:17
  679.7 27.1 %collective-permute-start.4 = (f32[384,2,128]{2,0,1:T(8,128)}, f32[384,2,128]{2,0,1:T(8,128)}, u32[]{:S(2)}, u32[]{:S(2)}) collective-permute-start(f32[384,2,128]{2,0,1:T(8,128)} %fusion.268), channel_id=1, source_target_pairs={{7,0},{0,1},{1,2},{2,3},{3,4},{4,5},{5,6},{6,7},{15,8},{8,9},{9,10... | collective-permute-start | bytes 1179656 | tf_op jit(solution)/shard_map/while/body/eval_jaxpr/ppermute | solution.py:17
  681.8 25.0 %collective-permute-start.5 = (f32[384,2,128]{2,0,1:T(8,128)}, f32[384,2,128]{2,0,1:T(8,128)}, u32[]{:S(2)}, u32[]{:S(2)}) collective-permute-start(f32[384,2,128]{2,0,1:T(8,128)} %fusion.269), channel_id=1, source_target_pairs={{7,0},{0,1},{1,2},{2,3},{3,4},{4,5},{5,6},{6,7},{15,8},{8,9},{9,10... | collective-permute-start | bytes 1179656 | tf_op jit(solution)/shard_map/while/body/eval_jaxpr/ppermute | solution.py:17
  681.8 22.9 %collective-permute-start.2 = (bf16[384,2,128]{2,0,1:T(8,128)(2,1)}, bf16[384,2,128]{2,0,1:T(8,128)(2,1)}, u32[]{:S(2)}, u32[]{:S(2)}) collective-permute-start(bf16[384,2,128]{2,0,1:T(8,128)(2,1)} %copy.191), channel_id=1, source_target_pairs={{7,0},{0,1},{1,2},{2,3},{3,4},{4,5},{5,6},{6,7},{15,8},{8,9},{9,10... | collective-permute-start | bytes 589832 | tf_op jit(solution)/shard_map/while/body/eval_jaxpr/ppermute | solution.py:17
  681.8 25.0 %collective-permute-start.3 = (bf16[384,2,128]{2,0,1:T(8,128)(2,1)}, bf16[384,2,128]{2,0,1:T(8,128)(2,1)}, u32[]{:S(2)}, u32[]{:S(2)}) collective-permute-start(bf16[384,2,128]{2,0,1:T(8,128)(2,1)} %copy.192), channel_id=1, source_target_pairs={{7,0},{0,1},{1,2},{2,3},{3,4},{4,5},{5,6},{6,7},{15,8},{8,9},{9,10... | collective-permute-start | bytes 589832 | tf_op jit(solution)/shard_map/while/body/eval_jaxpr/ppermute | solution.py:17
  716.2 26.2 %collective-permute-start.4 = (f32[384,2,128]{2,0,1:T(8,128)}, f32[384,2,128]{2,0,1:T(8,128)}, u32[]{:S(2)}, u32[]{:S(2)}) collective-permute-start(f32[384,2,128]{2,0,1:T(8,128)} %fusion.268), channel_id=1, source_target_pairs={{7,0},{0,1},{1,2},{2,3},{3,4},{4,5},{5,6},{6,7},{15,8},{8,9},{9,10... | collective-permute-start | bytes 1179656 | tf_op jit(solution)/shard_map/while/body/eval_jaxpr/ppermute | solution.py:17
  718.3 24.1 %collective-permute-start.5 = (f32[384,2,128]{2,0,1:T(8,128)}, f32[384,2,128]{2,0,1:T(8,128)}, u32[]{:S(2)}, u32[]{:S(2)}) collective-permute-start(f32[384,2,128]{2,0,1:T(8,128)} %fusion.269), channel_id=1, source_target_pairs={{7,0},{0,1},{1,2},{2,3},{3,4},{4,5},{5,6},{6,7},{15,8},{8,9},{9,10... | collective-permute-start | bytes 1179656 | tf_op jit(solution)/shard_map/while/body/eval_jaxpr/ppermute | solution.py:17
  718.3 22.0 %collective-permute-start.2 = (bf16[384,2,128]{2,0,1:T(8,128)(2,1)}, bf16[384,2,128]{2,0,1:T(8,128)(2,1)}, u32[]{:S(2)}, u32[]{:S(2)}) collective-permute-start(bf16[384,2,128]{2,0,1:T(8,128)(2,1)} %copy.191), channel_id=1, source_target_pairs={{7,0},{0,1},{1,2},{2,3},{3,4},{4,5},{5,6},{6,7},{15,8},{8,9},{9,10... | collective-permute-start | bytes 589832 | tf_op jit(solution)/shard_map/while/body/eval_jaxpr/ppermute | solution.py:17
  718.3 24.1 %collective-permute-start.3 = (bf16[384,2,128]{2,0,1:T(8,128)(2,1)}, bf16[384,2,128]{2,0,1:T(8,128)(2,1)}, u32[]{:S(2)}, u32[]{:S(2)}) collective-permute-start(bf16[384,2,128]{2,0,1:T(8,128)(2,1)} %copy.192), channel_id=1, source_target_pairs={{7,0},{0,1},{1,2},{2,3},{3,4},{4,5},{5,6},{6,7},{15,8},{8,9},{9,10... | collective-permute-start | bytes 589832 | tf_op jit(solution)/shard_map/while/body/eval_jaxpr/ppermute | solution.py:17
  752.2 8.5 %collective-permute-start.7 = (bf16[384,2,128]{0,2,1:T(8,128)(2,1)}, bf16[384,2,128]{0,2,1:T(8,128)(2,1)}, u32[]{:S(2)}, u32[]{:S(2)}) collective-permute-start(bf16[384,2,128]{0,2,1:T(8,128)(2,1)} %fusion.171), channel_id=1, source_target_pairs={{7,0},{0,1},{1,2},{2,3},{3,4},{4,5},{5,6},{6,7},{15,8},{8,9},{9,10... | collective-permute-start | bytes 589832 | tf_op jit(solution)/shard_map/ppermute | solution.py:17
  756.3 8.1 collective-permute-start.6
  (55 other events, 1569.7 us)
Sparse Core Ops, SparseCore 0:
  210.1 120.7 reduce-scatter.6
  333.7 76.8 all-gather.2
  462.4 137.8 reduce-scatter.4
where the time goes:
time: 816 us; the launch traced here: 810 us
  blocking collectives  209 us (26%)
  waiting for transfers between devices  195 us (24%)
  other arithmetic  142 us (17%)
  matrix products  110 us (13%)
  local copies, waits for them, and re-layouts  96.7 us (12%)
  starting transfers between devices  40.9 us (5%)
  between operations  17 us (2%)
    ppermute x44, waiting for transfers between devices, from_behind(): return lax.ppermute(block, axis, route)  194 us
    unnamed x2, blocking collectives  132 us
    while x63, local copies, waits for them, and re-layouts  53.4 us
    concatenate x3, other arithmetic, per_device(): jnp.concatenate([first_half, second_half], axis=-1).astype(jnp.bfloat16)  49.8 us
    reduce_sum x1, other arithmetic, norm_backward(): centre = mixed - jnp.mean(mixed, axis=-1, keepdims=True)  43.8 us
    all_gather x1, blocking collectives, per_device(): lax.all_gather(kernel, 'dp', axis=0, tiled=True)  41.1 us
    psum x1, blocking collectives, per_device(): lax.psum((proj_part, kernel_part, gain_part), 'tm')  35.7 us
    reduce_sum x4, other arithmetic, tap_products(): jnp.sum(grad_f * padded[tap:tap + frame_rows].astype(jnp.float32), axis=0)  28 us
  transfers between devices with their start and end apart: 51, of which 27 were waited for; matrix products, arithmetic and copies ran while one was open for 30% of the time, Pallas kernels for 0%

commit v1 on v0

--- a/solution.py
+++ b/solution.py
@@ -9,6 +9,15 @@
 KW = 31
 NEG_FILL = -1e30
 NORM_EPS = 1e-05
+
+
+def place_the_strings(packet):
+    return jnp.concatenate(
+        lax.all_to_all(
+            jnp.stack([packet] * lax.axis_size("dp")), "dp", split_axis=0, concat_axis=0
+        ),
+        axis=0,
+    )
 
 
 def from_behind(block, axis, distance):
@@ -102,7 +111,7 @@
     length = lengths[0]
     full_proj, full_kernel, full_gain = (
         lax.all_gather(projection, "dp", axis=0, tiled=True),
-        lax.all_gather(kernel, "dp", axis=0, tiled=True),
+        place_the_strings(kernel),
         lax.all_gather(norm_gain, "dp", axis=0, tiled=True),
     )
     query_heads = queries[0].reshape(frame_rows, HEADS, HDIM)

time: 816 us -> 776 us (0.951)
  blocking collectives: 209 us -> 163 us
  starting transfers between devices: 40.9 us -> 53.8 us
    all_gather x1 -> x0, blocking collectives: 41.1 us -> none  [per_device(): lax.all_gather(kernel, 'dp', axis=0, tiled=True)]
    all_to_all x0 -> x1, starting transfers between devices: none -> 11.6 us  [place_the_strings(): lax.all_to_all(jnp.stack([packet] * lax.axis_size('dp')), 'dp', split_axi...]
    ppermute x44, starting transfers between devices: 20.5 us -> 31 us  [from_behind(): return lax.ppermute(block, axis, route)]
    reduce_scatter x1, starting transfers between devices: 9.55 us -> 0.21 us  [per_device(): lax.psum_scatter(lax.dot_general(upstream_rows, attended_flat, (((0,), (0...]
    unnamed x127 -> x188, local copies, waits for them, and re-layouts: 24.8 us -> 26.5 us
  transfers between devices with their start and end apart: 51 -> 52, of which waited for: 27 -> 26; matrix products, arithmetic and copies ran while one was open for 30% -> 31% of each run, Pallas kernels for 0% -> 0%
where the time goes in v1:
time: 776 us; the launch traced here: 768 us
  waiting for transfers between devices  191 us (25%)
  blocking collectives  163 us (21%)
  other arithmetic  136 us (18%)
  matrix products  110 us (14%)
  local copies, waits for them, and re-layouts  97 us (12%)
  starting transfers between devices  53.8 us (7%)
  between operations  17.3 us (2%)
    ppermute x44, waiting for transfers between devices, from_behind(): return lax.ppermute(block, axis, route)  190 us
    unnamed x2, blocking collectives  128 us
    while x63, local copies, waits for them, and re-layouts  53.4 us
    concatenate x3, other arithmetic, per_device(): jnp.concatenate([first_half, second_half], axis=-1).astype(jnp.bfloat16)  45.9 us
    reduce_sum x1, other arithmetic, norm_backward(): centre = mixed - jnp.mean(mixed, axis=-1, keepdims=True)  41.9 us
    psum x1, blocking collectives, per_device(): lax.psum((proj_part, kernel_part, gain_part), 'tm')  35.6 us
    ppermute x44, starting transfers between devices, from_behind(): return lax.ppermute(block, axis, route)  31 us
    reduce_sum x4, other arithmetic, tap_products(): jnp.sum(grad_f * padded[tap:tap + frame_rows].astype(jnp.float32), axis=0)  27.9 us
  transfers between devices with their start and end apart: 52, of which 26 were waited for; matrix products, arithmetic and copies ran while one was open for 31% of the time, Pallas kernels for 0%

profile of v1, /device:TPU:4, one launch (start us, length us, event | category | flops | bytes accessed | tf_op | source)
XLA Modules:
  0.0 768.0 jit_solution(11246165425404114610)
XLA Ops:
  8.9 11.6 %all-to-all-start = ((bf16[32,2,992]{2,1,0:T(2,128)(2,1)}), bf16[32,2,992]{2,1,0:T(2,128)(2,1)}, u32[]{:S(2)}, u32[]{:S(2)}) async-start(bf16[32,2,992]{2,1,0:T(2,128)(2,1)} %reshape.197), calls=%async_computation.1 | async-start | bytes 262144 | tf_op jit(solution)/shard_map/all_to_all | solution.py:16
  21.3 2.9 fusion.18
  26.0 3.1 collective-permute-start.8
  32.0 64.3 %all-reduce = bf16[2048]{0:T(1024)(128)(2,1)S(1)} all-reduce(bf16[2048]{0:T(1024)(128)(2,1)S(1)} %dynamic-update-slice), channel_id=1, replica_groups=mesh['dp'=32,'tm'=8] {'dp'}, use_global_device_ids=true, to_apply=%add | all-reduce | flops 2048 | bytes 8192
  100.2 41.9 %fusion.190 = (f32[384]{0:T(512)S(1)}, f32[384,2048]{1,0:T(8,128)S(1)}) fusion(f32[2048]{0:T(1024)S(1)} %bitcast.232, bf16[15,2048]{1,0:T(8,128)(2,1)S(1)} %collective-permute-done.9, bf16[384,2048]{1,0:T(8,128)(2,1)} %copy-done.3, f32[2048]{0:T(1024)S(1)} %bitcast.234, f32[2048]{0:T(1024)S(1)} %bitcast.236, f32[2048]{0:T(1024)S(1)} %bitcast.238, ...), kind=kLoop, calls=%fused_computation.373 | loop fusion | flops 143916672 | bytes 5096960 | tf_op jit(solution)/shard_map/reduce_sum | solution.py:76
  142.9 3.1 multiply_reduce_fusion
  146.1 12.3 %fusion.98 = (f32[2048]{0:T(1024)}, f32[2048]{0:T(1024)}, f32[2048]{0:T(1024)}, f32[2048]{0:T(1024)}, f32[2048]{0:T(1024)}, /*index=5*/f32[2048]{0:T(1024)}, f32...) fusion(bf16[15,2048]{1,0:T(8,128)(2,1)S(1)} %collective-permute-done.9, ...), kind=kLoop, calls=%fused_computation.234 | loop fusion | flops 49526784 | bytes 9586688 | tf_op jit(solution)/shard_map/reduce_sum | solution.py:68
  158.4 7.3 fusion.97
  165.7 4.7 fusion.82
  170.5 3.6 fusion.81
  174.1 3.5 stack.163
  191.9 95.2 %while.48 = (s32[]{:T(128)}, bf16[384,2,128]{2,0,1:T(8,128)(2,1)}, bf16[384,2,128]{2,0,1:T(8,128)(2,1)}, f32[2,384]{1,0:T(2,128)S(1)}, f32[2,384]{1,0:T(2,128)S(...) while((s32[]{:T(128)}, bf16[384,2,128]{2,0,1:T(8,128)(2,1)}, ...), condition=%wide.region_3.4_spmd.clone, body=%wide.region_0.3_spmd.clone.sunk | while | flops 530552064 | bytes 12043402 | solution.py:158
  192.8 2.5 collective-permute-start
  196.9 2.6 collective-permute-start.1
  201.8 3.2 fusion.255
  212.9 3.3 fusion.255
  216.2 2.3 collective-permute-done.1
  221.1 2.1 collective-permute-start.1
  225.5 3.3 fusion.255
  228.8 2.9 collective-permute-done.1
  237.8 3.3 fusion.255
  241.1 2.4 collective-permute-done
  243.5 4.2 collective-permute-done.1
  253.3 3.3 fusion.255
  258.6 3.4 collective-permute-done.1
  266.8 3.3 fusion.255
  270.1 2.8 collective-permute-done
  272.9 2.5 collective-permute-done.1
  280.2 3.3 fusion.255
  292.7 5.2 collective-permute-start.11
  301.1 63.2 %all-reduce.1 = f32[2048]{0:T(1024)} all-reduce(f32[2048]{0:T(1024)} %get-tuple-element.733), channel_id=4, replica_groups=mesh['dp'=32,'tm'=8] {'dp'}, use_global_device_ids=true, to_apply=%region_48.49.clone | all-reduce | flops 2048 | bytes 16384
  365.9 42.8 %fusion.104 = (bf16[1,384,2048]{2,1,0:T(8,128)(2,1)S(1)}, f32[384,2048]{1,0:T(8,128)S(1)}) fusion(bf16[384,4096]{1,0:T(8,128)(2,1)} %bitcast.215, f32[384]{0:T(512)S(1)} %copy-done.78, f32[2048]{0:T(1024)S(1)} %bitcast.233, bf16[384,2048]{1,0:T(8,128)(2,1)} %copy-done.5, bf16[15,2048]{1,0:T(8,128)(2,1)} %collective-permute-done.11, f32[2048]{0:T(1024)S(1)} %bitcast.235, ...), kind=kLoop, calls=%fused_computation.250 | loop fusion | flops 148635648 | bytes 8242688 | tf_op jit(solution)/shard_map/concatenate | solution.py:237
  413.3 3.0 fusion.174
  418.2 3.2 convolution_bitcast_fusion.4
  424.1 276.9 %while.49 = (s32[]{:T(128)}, bf16[384,2,128]{2,0,1:T(8,128)(2,1)}, bf16[384,2,128]{2,0,1:T(8,128)(2,1)}, f32[384,2,128]{2,0,1:T(8,128)}, f32[384,2,128]{2,0,1:T(...) while((s32[]{:T(128)}, bf16[384,2,128]{2,0,1:T(8,128)(2,1)}, ...), condition=%wide.region_7.8_spmd.clone, body=%wide.region_6.7_spmd.clone.sunk | while | flops 380240640 | bytes 16915696 | solution.py:207
  431.6 2.1 fusion.268
  439.0 2.5 collective-permute-start.2
  441.6 2.2 fusion.270
  443.8 17.0 %collective-permute-done.2 = bf16[384,2,128]{2,0,1:T(8,128)(2,1)} collective-permute-done((bf16[384,2,128]{2,0,1:T(8,128)(2,1)}, bf16[384,2,128]{2,0,1:T(8,128)(2,1)}, u32[]{:S(2)}, u32[]{:S(2)}) %collective-permute-start.2) | collective-permute-done | bytes 196640 | tf_op jit(solution)/shard_map/while/body/eval_jaxpr/ppermute | solution.py:26
  460.8 3.0 collective-permute-done.3
  471.1 2.2 fusion.268
  475.4 2.2 collective-permute-start.5
  480.2 2.3 fusion.270
  482.5 26.3 %collective-permute-done.2 = bf16[384,2,128]{2,0,1:T(8,128)(2,1)} collective-permute-done((bf16[384,2,128]{2,0,1:T(8,128)(2,1)}, bf16[384,2,128]{2,0,1:T(8,128)(2,1)}, u32[]{:S(2)}, u32[]{:S(2)}) %collective-permute-start.2) | collective-permute-done | bytes 196640 | tf_op jit(solution)/shard_map/while/body/eval_jaxpr/ppermute | solution.py:26
  508.8 3.5 collective-permute-done.3
  519.6 2.1 fusion.268
  527.6 2.3 fusion.270
  529.9 20.3 %collective-permute-done.2 = bf16[384,2,128]{2,0,1:T(8,128)(2,1)} collective-permute-done((bf16[384,2,128]{2,0,1:T(8,128)(2,1)}, bf16[384,2,128]{2,0,1:T(8,128)(2,1)}, u32[]{:S(2)}, u32[]{:S(2)}) %collective-permute-start.2) | collective-permute-done | bytes 196640 | tf_op jit(solution)/shard_map/while/body/eval_jaxpr/ppermute | solution.py:26
  550.2 2.7 collective-permute-done.3
  564.5 2.6 collective-permute-start.3
  567.1 2.3 fusion.270
  569.4 19.7 %collective-permute-done.2 = bf16[384,2,128]{2,0,1:T(8,128)(2,1)} collective-permute-done((bf16[384,2,128]{2,0,1:T(8,128)(2,1)}, bf16[384,2,128]{2,0,1:T(8,128)(2,1)}, u32[]{:S(2)}, u32[]{:S(2)}) %collective-permute-start.2) | collective-permute-done | bytes 196640 | tf_op jit(solution)/shard_map/while/body/eval_jaxpr/ppermute | solution.py:26
  604.3 2.3 fusion.270
  606.6 20.0 %collective-permute-done.2 = bf16[384,2,128]{2,0,1:T(8,128)(2,1)} collective-permute-done((bf16[384,2,128]{2,0,1:T(8,128)(2,1)}, bf16[384,2,128]{2,0,1:T(8,128)(2,1)}, u32[]{:S(2)}, u32[]{:S(2)}) %collective-permute-start.2) | collective-permute-done | bytes 196640 | tf_op jit(solution)/shard_map/while/body/eval_jaxpr/ppermute | solution.py:26
  636.0 2.1 fusion.268
  640.6 2.3 fusion.270
  642.9 20.2 %collective-permute-done.2 = bf16[384,2,128]{2,0,1:T(8,128)(2,1)} collective-permute-done((bf16[384,2,128]{2,0,1:T(8,128)(2,1)}, bf16[384,2,128]{2,0,1:T(8,128)(2,1)}, u32[]{:S(2)}, u32[]{:S(2)}) %collective-permute-start.2) | collective-permute-done | bytes 196640 | tf_op jit(solution)/shard_map/while/body/eval_jaxpr/ppermute | solution.py:26
  676.8 2.3 fusion.270
  679.2 19.7 %collective-permute-done.2 = bf16[384,2,128]{2,0,1:T(8,128)(2,1)} collective-permute-done((bf16[384,2,128]{2,0,1:T(8,128)(2,1)}, bf16[384,2,128]{2,0,1:T(8,128)(2,1)}, u32[]{:S(2)}, u32[]{:S(2)}) %collective-permute-start.2) | collective-permute-done | bytes 196640 | tf_op jit(solution)/shard_map/while/body/eval_jaxpr/ppermute | solution.py:26
  701.0 2.4 convolution_multiply_fusion.2
  703.4 2.6 copy.161
  708.1 2.6 fusion.171
  712.7 2.2 fusion.170
  724.9 35.6 %all-reduce.4 = (bf16[128,256]{0,1:T(8,128)(2,1)S(1)}, f32[64,31]{0,1:T(8,128)}, f32[64]{0:T(128)}) all-reduce(f32[128,256]{0,1:T(8,128)} %reduce-scatter.5.cloned.1.call-done, f32[64,31]{0,1:T(8,128)S(1)} %copy-done.71, f32[64]{0:T(128)} %dynamic-slice.2), channel_id=1, replica_groups=mesh['dp'=32,'tm'=8] {'tm'}, use_global_device_ids=true, to_apply=%region_9.10 | all-reduce | flops 34816 | bytes 212992 | tf_op jit(solution)/shard_map/psum | solution.py:254
  (430 shorter events, 193.4 us)
Async XLA Ops:
  7.2 406.1 %copy-start = (bf16[1,384,4096]{2,1,0:T(8,128)(2,1)S(1)}, bf16[1,384,4096]{2,1,0:T(8,128)(2,1)}, u32[]{:S(2)}) copy-start(bf16[1,384,4096]{2,1,0:T(8,128)(2,1)} %param.19) | copy-start | bytes 9437188
  8.9 87.4 %all-to-all-start = ((bf16[32,2,992]{2,1,0:T(2,128)(2,1)}), bf16[32,2,992]{2,1,0:T(2,128)(2,1)}, u32[]{:S(2)}, u32[]{:S(2)}) async-start(bf16[32,2,992]{2,1,0:T(2,128)(2,1)} %reshape.197), calls=%async_computation.1 | async-start | bytes 262144 | tf_op jit(solution)/shard_map/all_to_all | solution.py:16
  20.6 391.2 %reduce-scatter.7.cloned.1.call-start = ((), (), s32[]{:S(2)}) async-start(), calls=%async_computation.5 | async-start | bytes 1081344
  21.3 121.6 %copy-start.77 = (f32[384]{0:T(512)}, f32[384]{0:T(512)S(1)}, u32[]{:S(2)}) copy-start(f32[384]{0:T(512)S(1)} %fusion.183) | copy-start | bytes 4612
  26.0 74.1 %collective-permute-start.8 = (bf16[15,2048]{1,0:T(8,128)(2,1)}, bf16[15,2048]{1,0:T(8,128)(2,1)S(1)}, u32[]{:S(2)}, u32[]{:S(2)}) collective-permute-start(bf16[15,2048]{1,0:T(8,128)(2,1)} %get-tuple-element.826), channel_id=1, source_target_pairs={{0,1},{1,2},{2,3},{3,4},{4,5},{5,6},{6,7},{8,9},{9,10},{10,11},{11... | collective-permute-start | bytes 184328 | tf_op jit(solution)/shard_map/ppermute | solution.py:37
  29.1 71.0 %collective-permute-start.9 = (bf16[15,2048]{1,0:T(8,128)(2,1)}, bf16[15,2048]{1,0:T(8,128)(2,1)S(1)}, u32[]{:S(2)}, u32[]{:S(2)}) collective-permute-start(bf16[15,2048]{1,0:T(8,128)(2,1)} %get-tuple-element.827), channel_id=1, source_target_pairs={{1,0},{2,1},{3,2},{4,3},{5,4},{6,5},{7,6},{9,8},{10,9},{11,10},{12... | collective-permute-start | bytes 184328 | tf_op jit(solution)/shard_map/ppermute | solution.py:39
  178.9 234.4 %all-gather.2.cloned.1.call-start = ((), (), s32[]{:S(2)}) async-start(), calls=%async_computation.3 | async-start | bytes 2162688 | tf_op jit(solution)/shard_map/all_gather | solution.py:113
  179.7 545.2 %reduce-scatter.5.cloned.1.call-start = ((), (), s32[]{:S(2)}) async-start(), calls=%async_computation.4 | async-start | bytes 4325376 | tf_op jit(solution)/shard_map/reduce_scatter | solution.py:239
  192.8 12.2 %collective-permute-start = (bf16[384,2,128]{2,0,1:T(8,128)(2,1)S(1)}, bf16[384,2,128]{2,0,1:T(8,128)(2,1)}, u32[]{:S(2)}, u32[]{:S(2)}) collective-permute-start(bf16[384,2,128]{2,0,1:T(8,128)(2,1)S(1)} %copy.207), channel_id=1, source_target_pairs={{7,0},{0,1},{1,2},{2,3},{3,4},{4,5},{5,6},{6,7},{15,8},{8,9},{9,10... | collective-permute-start | bytes 589832 | tf_op jit(solution)/shard_map/while/body/eval_jaxpr/ppermute | solution.py:26
  196.9 8.1 %collective-permute-start.1 = (bf16[384,2,128]{2,0,1:T(8,128)(2,1)}, bf16[384,2,128]{2,0,1:T(8,128)(2,1)}, u32[]{:S(2)}, u32[]{:S(2)}) collective-permute-start(bf16[384,2,128]{2,0,1:T(8,128)(2,1)} %copy.208), channel_id=1, source_target_pairs={{7,0},{0,1},{1,2},{2,3},{3,4},{4,5},{5,6},{6,7},{15,8},{8,9},{9,10... | collective-permute-start | bytes 589832 | tf_op jit(solution)/shard_map/while/body/eval_jaxpr/ppermute | solution.py:26
  206.0 10.3 %collective-permute-start = (bf16[384,2,128]{2,0,1:T(8,128)(2,1)S(1)}, bf16[384,2,128]{2,0,1:T(8,128)(2,1)}, u32[]{:S(2)}, u32[]{:S(2)}) collective-permute-start(bf16[384,2,128]{2,0,1:T(8,128)(2,1)S(1)} %copy.207), channel_id=1, source_target_pairs={{7,0},{0,1},{1,2},{2,3},{3,4},{4,5},{5,6},{6,7},{15,8},{8,9},{9,10... | collective-permute-start | bytes 589832 | tf_op jit(solution)/shard_map/while/body/eval_jaxpr/ppermute | solution.py:26
  209.3 9.2 %collective-permute-start.1 = (bf16[384,2,128]{2,0,1:T(8,128)(2,1)}, bf16[384,2,128]{2,0,1:T(8,128)(2,1)}, u32[]{:S(2)}, u32[]{:S(2)}) collective-permute-start(bf16[384,2,128]{2,0,1:T(8,128)(2,1)} %copy.208), channel_id=1, source_target_pairs={{7,0},{0,1},{1,2},{2,3},{3,4},{4,5},{5,6},{6,7},{15,8},{8,9},{9,10... | collective-permute-start | bytes 589832 | tf_op jit(solution)/shard_map/while/body/eval_jaxpr/ppermute | solution.py:26
  219.5 9.4 %collective-permute-start = (bf16[384,2,128]{2,0,1:T(8,128)(2,1)S(1)}, bf16[384,2,128]{2,0,1:T(8,128)(2,1)}, u32[]{:S(2)}, u32[]{:S(2)}) collective-permute-start(bf16[384,2,128]{2,0,1:T(8,128)(2,1)S(1)} %copy.207), channel_id=1, source_target_pairs={{7,0},{0,1},{1,2},{2,3},{3,4},{4,5},{5,6},{6,7},{15,8},{8,9},{9,10... | collective-permute-start | bytes 589832 | tf_op jit(solution)/shard_map/while/body/eval_jaxpr/ppermute | solution.py:26
  221.1 10.6 %collective-permute-start.1 = (bf16[384,2,128]{2,0,1:T(8,128)(2,1)}, bf16[384,2,128]{2,0,1:T(8,128)(2,1)}, u32[]{:S(2)}, u32[]{:S(2)}) collective-permute-start(bf16[384,2,128]{2,0,1:T(8,128)(2,1)} %copy.208), channel_id=1, source_target_pairs={{7,0},{0,1},{1,2},{2,3},{3,4},{4,5},{5,6},{6,7},{15,8},{8,9},{9,10... | collective-permute-start | bytes 589832 | tf_op jit(solution)/shard_map/while/body/eval_jaxpr/ppermute | solution.py:26
  232.7 10.8 %collective-permute-start = (bf16[384,2,128]{2,0,1:T(8,128)(2,1)S(1)}, bf16[384,2,128]{2,0,1:T(8,128)(2,1)}, u32[]{:S(2)}, u32[]{:S(2)}) collective-permute-start(bf16[384,2,128]{2,0,1:T(8,128)(2,1)S(1)} %copy.207), channel_id=1, source_target_pairs={{7,0},{0,1},{1,2},{2,3},{3,4},{4,5},{5,6},{6,7},{15,8},{8,9},{9,10... | collective-permute-start | bytes 589832 | tf_op jit(solution)/shard_map/while/body/eval_jaxpr/ppermute | solution.py:26
  234.3 13.4 %collective-permute-start.1 = (bf16[384,2,128]{2,0,1:T(8,128)(2,1)}, bf16[384,2,128]{2,0,1:T(8,128)(2,1)}, u32[]{:S(2)}, u32[]{:S(2)}) collective-permute-start(bf16[384,2,128]{2,0,1:T(8,128)(2,1)} %copy.208), channel_id=1, source_target_pairs={{7,0},{0,1},{1,2},{2,3},{3,4},{4,5},{5,6},{6,7},{15,8},{8,9},{9,10... | collective-permute-start | bytes 589832 | tf_op jit(solution)/shard_map/while/body/eval_jaxpr/ppermute | solution.py:26
  248.7 10.0 %collective-permute-start = (bf16[384,2,128]{2,0,1:T(8,128)(2,1)S(1)}, bf16[384,2,128]{2,0,1:T(8,128)(2,1)}, u32[]{:S(2)}, u32[]{:S(2)}) collective-permute-start(bf16[384,2,128]{2,0,1:T(8,128)(2,1)S(1)} %copy.207), channel_id=1, source_target_pairs={{7,0},{0,1},{1,2},{2,3},{3,4},{4,5},{5,6},{6,7},{15,8},{8,9},{9,10... | collective-permute-start | bytes 589832 | tf_op jit(solution)/shard_map/while/body/eval_jaxpr/ppermute | solution.py:26
  250.3 11.7 %collective-permute-start.1 = (bf16[384,2,128]{2,0,1:T(8,128)(2,1)}, bf16[384,2,128]{2,0,1:T(8,128)(2,1)}, u32[]{:S(2)}, u32[]{:S(2)}) collective-permute-start(bf16[384,2,128]{2,0,1:T(8,128)(2,1)} %copy.208), channel_id=1, source_target_pairs={{7,0},{0,1},{1,2},{2,3},{3,4},{4,5},{5,6},{6,7},{15,8},{8,9},{9,10... | collective-permute-start | bytes 589832 | tf_op jit(solution)/shard_map/while/body/eval_jaxpr/ppermute | solution.py:26
  262.9 10.0 %collective-permute-start = (bf16[384,2,128]{2,0,1:T(8,128)(2,1)S(1)}, bf16[384,2,128]{2,0,1:T(8,128)(2,1)}, u32[]{:S(2)}, u32[]{:S(2)}) collective-permute-start(bf16[384,2,128]{2,0,1:T(8,128)(2,1)S(1)} %copy.207), channel_id=1, source_target_pairs={{7,0},{0,1},{1,2},{2,3},{3,4},{4,5},{5,6},{6,7},{15,8},{8,9},{9,10... | collective-permute-start | bytes 589832 | tf_op jit(solution)/shard_map/while/body/eval_jaxpr/ppermute | solution.py:26
  264.6 10.9 %collective-permute-start.1 = (bf16[384,2,128]{2,0,1:T(8,128)(2,1)}, bf16[384,2,128]{2,0,1:T(8,128)(2,1)}, u32[]{:S(2)}, u32[]{:S(2)}) collective-permute-start(bf16[384,2,128]{2,0,1:T(8,128)(2,1)} %copy.208), channel_id=1, source_target_pairs={{7,0},{0,1},{1,2},{2,3},{3,4},{4,5},{5,6},{6,7},{15,8},{8,9},{9,10... | collective-permute-start | bytes 589832 | tf_op jit(solution)/shard_map/while/body/eval_jaxpr/ppermute | solution.py:26
  276.4 8.6 %collective-permute-start = (bf16[384,2,128]{2,0,1:T(8,128)(2,1)S(1)}, bf16[384,2,128]{2,0,1:T(8,128)(2,1)}, u32[]{:S(2)}, u32[]{:S(2)}) collective-permute-start(bf16[384,2,128]{2,0,1:T(8,128)(2,1)S(1)} %copy.207), channel_id=1, source_target_pairs={{7,0},{0,1},{1,2},{2,3},{3,4},{4,5},{5,6},{6,7},{15,8},{8,9},{9,10... | collective-permute-start | bytes 589832 | tf_op jit(solution)/shard_map/while/body/eval_jaxpr/ppermute | solution.py:26
  278.0 9.1 %collective-permute-start.1 = (bf16[384,2,128]{2,0,1:T(8,128)(2,1)}, bf16[384,2,128]{2,0,1:T(8,128)(2,1)}, u32[]{:S(2)}, u32[]{:S(2)}) collective-permute-start(bf16[384,2,128]{2,0,1:T(8,128)(2,1)} %copy.208), channel_id=1, source_target_pairs={{7,0},{0,1},{1,2},{2,3},{3,4},{4,5},{5,6},{6,7},{15,8},{8,9},{9,10... | collective-permute-start | bytes 589832 | tf_op jit(solution)/shard_map/while/body/eval_jaxpr/ppermute | solution.py:26
  287.1 78.6 %copy-start.25 = (f32[2048,1]{0,1:T(1,128)S(1)}, f32[2048,1]{0,1:T(1,128)}, u32[]{:S(2)}) copy-start(f32[2048,1]{0,1:T(1,128)} %copy-done.24) | copy-start | bytes 24580
  287.1 78.6 %copy-start.27 = (f32[2048,1]{0,1:T(1,128)S(1)}, f32[2048,1]{0,1:T(1,128)}, u32[]{:S(2)}) copy-start(f32[2048,1]{0,1:T(1,128)} %copy-done.26) | copy-start | bytes 24580
  287.1 78.6 %copy-start.29 = (f32[2048,1]{0,1:T(1,128)S(1)}, f32[2048,1]{0,1:T(1,128)}, u32[]{:S(2)}) copy-start(f32[2048,1]{0,1:T(1,128)} %copy-done.28) | copy-start | bytes 24580
  287.1 78.6 %copy-start.31 = (f32[2048,1]{0,1:T(1,128)S(1)}, f32[2048,1]{0,1:T(1,128)}, u32[]{:S(2)}) copy-start(f32[2048,1]{0,1:T(1,128)} %copy-done.30) | copy-start | bytes 24580
  287.1 78.6 %copy-start.33 = (f32[2048,1]{0,1:T(1,128)S(1)}, f32[2048,1]{0,1:T(1,128)}, u32[]{:S(2)}) copy-start(f32[2048,1]{0,1:T(1,128)} %copy-done.32) | copy-start | bytes 24580
  287.1 78.6 %copy-start.35 = (f32[2048,1]{0,1:T(1,128)S(1)}, f32[2048,1]{0,1:T(1,128)}, u32[]{:S(2)}) copy-start(f32[2048,1]{0,1:T(1,128)} %copy-done.34) | copy-start | bytes 24580
  287.1 78.6 %copy-start.37 = (f32[2048,1]{0,1:T(1,128)S(1)}, f32[2048,1]{0,1:T(1,128)}, u32[]{:S(2)}) copy-start(f32[2048,1]{0,1:T(1,128)} %copy-done.36) | copy-start | bytes 24580
  287.1 78.6 %copy-start.39 = (f32[2048,1]{0,1:T(1,128)S(1)}, f32[2048,1]{0,1:T(1,128)}, u32[]{:S(2)}) copy-start(f32[2048,1]{0,1:T(1,128)} %copy-done.38) | copy-start | bytes 24580
  287.1 78.6 %copy-start.41 = (f32[2048,1]{0,1:T(1,128)S(1)}, f32[2048,1]{0,1:T(1,128)}, u32[]{:S(2)}) copy-start(f32[2048,1]{0,1:T(1,128)} %copy-done.40) | copy-start | bytes 24580
  287.2 78.6 %copy-start.43 = (f32[2048,1]{0,1:T(1,128)S(1)}, f32[2048,1]{0,1:T(1,128)}, u32[]{:S(2)}) copy-start(f32[2048,1]{0,1:T(1,128)} %copy-done.42) | copy-start | bytes 24580
  291.4 74.2 %collective-permute-start.10 = (bf16[15,2048]{1,0:T(8,128)(2,1)}, bf16[15,2048]{1,0:T(8,128)(2,1)}, u32[]{:S(2)}, u32[]{:S(2)}) collective-permute-start(bf16[15,2048]{1,0:T(8,128)(2,1)} %get-tuple-element.824), channel_id=1, source_target_pairs={{1,0},{2,1},{3,2},{4,3},{5,4},{6,5},{7,6},{9,8},{10,9},{11,10},{12... | collective-permute-start | bytes 184328 | tf_op jit(solution)/shard_map/ppermute | solution.py:39
  292.7 72.9 %collective-permute-start.11 = (bf16[15,2048]{1,0:T(8,128)(2,1)}, bf16[15,2048]{1,0:T(8,128)(2,1)}, u32[]{:S(2)}, u32[]{:S(2)}) collective-permute-start(bf16[15,2048]{1,0:T(8,128)(2,1)} %get-tuple-element.825), channel_id=1, source_target_pairs={{0,1},{1,2},{2,3},{3,4},{4,5},{5,6},{6,7},{8,9},{9,10},{10,11},{11... | collective-permute-start | bytes 184328 | tf_op jit(solution)/shard_map/ppermute | solution.py:37
  433.8 30.1 %collective-permute-start.4 = (f32[384,2,128]{2,0,1:T(8,128)}, f32[384,2,128]{2,0,1:T(8,128)}, u32[]{:S(2)}, u32[]{:S(2)}) collective-permute-start(f32[384,2,128]{2,0,1:T(8,128)} %fusion.268), channel_id=1, source_target_pairs={{7,0},{0,1},{1,2},{2,3},{3,4},{4,5},{5,6},{6,7},{15,8},{8,9},{9,10... | collective-permute-start | bytes 1179656 | tf_op jit(solution)/shard_map/while/body/eval_jaxpr/ppermute | solution.py:26
  437.5 26.3 %collective-permute-start.5 = (f32[384,2,128]{2,0,1:T(8,128)}, f32[384,2,128]{2,0,1:T(8,128)}, u32[]{:S(2)}, u32[]{:S(2)}) collective-permute-start(f32[384,2,128]{2,0,1:T(8,128)} %fusion.269), channel_id=1, source_target_pairs={{7,0},{0,1},{1,2},{2,3},{3,4},{4,5},{5,6},{6,7},{15,8},{8,9},{9,10... | collective-permute-start | bytes 1179656 | tf_op jit(solution)/shard_map/while/body/eval_jaxpr/ppermute | solution.py:26
  439.0 21.8 %collective-permute-start.2 = (bf16[384,2,128]{2,0,1:T(8,128)(2,1)}, bf16[384,2,128]{2,0,1:T(8,128)(2,1)}, u32[]{:S(2)}, u32[]{:S(2)}) collective-permute-start(bf16[384,2,128]{2,0,1:T(8,128)(2,1)} %copy.225), channel_id=1, source_target_pairs={{7,0},{0,1},{1,2},{2,3},{3,4},{4,5},{5,6},{6,7},{15,8},{8,9},{9,10... | collective-permute-start | bytes 589832 | tf_op jit(solution)/shard_map/while/body/eval_jaxpr/ppermute | solution.py:26
  441.6 22.2 %collective-permute-start.3 = (bf16[384,2,128]{2,0,1:T(8,128)(2,1)}, bf16[384,2,128]{2,0,1:T(8,128)(2,1)}, u32[]{:S(2)}, u32[]{:S(2)}) collective-permute-start(bf16[384,2,128]{2,0,1:T(8,128)(2,1)} %copy.226), channel_id=1, source_target_pairs={{7,0},{0,1},{1,2},{2,3},{3,4},{4,5},{5,6},{6,7},{15,8},{8,9},{9,10... | collective-permute-start | bytes 589832 | tf_op jit(solution)/shard_map/while/body/eval_jaxpr/ppermute | solution.py:26
  473.3 39.0 %collective-permute-start.4 = (f32[384,2,128]{2,0,1:T(8,128)}, f32[384,2,128]{2,0,1:T(8,128)}, u32[]{:S(2)}, u32[]{:S(2)}) collective-permute-start(f32[384,2,128]{2,0,1:T(8,128)} %fusion.268), channel_id=1, source_target_pairs={{7,0},{0,1},{1,2},{2,3},{3,4},{4,5},{5,6},{6,7},{15,8},{8,9},{9,10... | collective-permute-start | bytes 1179656 | tf_op jit(solution)/shard_map/while/body/eval_jaxpr/ppermute | solution.py:26
  475.4 36.9 %collective-permute-start.5 = (f32[384,2,128]{2,0,1:T(8,128)}, f32[384,2,128]{2,0,1:T(8,128)}, u32[]{:S(2)}, u32[]{:S(2)}) collective-permute-start(f32[384,2,128]{2,0,1:T(8,128)} %fusion.269), channel_id=1, source_target_pairs={{7,0},{0,1},{1,2},{2,3},{3,4},{4,5},{5,6},{6,7},{15,8},{8,9},{9,10... | collective-permute-start | bytes 1179656 | tf_op jit(solution)/shard_map/while/body/eval_jaxpr/ppermute | solution.py:26
  477.6 31.2 %collective-permute-start.2 = (bf16[384,2,128]{2,0,1:T(8,128)(2,1)}, bf16[384,2,128]{2,0,1:T(8,128)(2,1)}, u32[]{:S(2)}, u32[]{:S(2)}) collective-permute-start(bf16[384,2,128]{2,0,1:T(8,128)(2,1)} %copy.225), channel_id=1, source_target_pairs={{7,0},{0,1},{1,2},{2,3},{3,4},{4,5},{5,6},{6,7},{15,8},{8,9},{9,10... | collective-permute-start | bytes 589832 | tf_op jit(solution)/shard_map/while/body/eval_jaxpr/ppermute | solution.py:26
  479.0 33.3 %collective-permute-start.3 = (bf16[384,2,128]{2,0,1:T(8,128)(2,1)}, bf16[384,2,128]{2,0,1:T(8,128)(2,1)}, u32[]{:S(2)}, u32[]{:S(2)}) collective-permute-start(bf16[384,2,128]{2,0,1:T(8,128)(2,1)} %copy.226), channel_id=1, source_target_pairs={{7,0},{0,1},{1,2},{2,3},{3,4},{4,5},{5,6},{6,7},{15,8},{8,9},{9,10... | collective-permute-start | bytes 589832 | tf_op jit(solution)/shard_map/while/body/eval_jaxpr/ppermute | solution.py:26
  521.7 31.1 %collective-permute-start.4 = (f32[384,2,128]{2,0,1:T(8,128)}, f32[384,2,128]{2,0,1:T(8,128)}, u32[]{:S(2)}, u32[]{:S(2)}) collective-permute-start(f32[384,2,128]{2,0,1:T(8,128)} %fusion.268), channel_id=1, source_target_pairs={{7,0},{0,1},{1,2},{2,3},{3,4},{4,5},{5,6},{6,7},{15,8},{8,9},{9,10... | collective-permute-start | bytes 1179656 | tf_op jit(solution)/shard_map/while/body/eval_jaxpr/ppermute | solution.py:26
  523.9 29.0 %collective-permute-start.5 = (f32[384,2,128]{2,0,1:T(8,128)}, f32[384,2,128]{2,0,1:T(8,128)}, u32[]{:S(2)}, u32[]{:S(2)}) collective-permute-start(f32[384,2,128]{2,0,1:T(8,128)} %fusion.269), channel_id=1, source_target_pairs={{7,0},{0,1},{1,2},{2,3},{3,4},{4,5},{5,6},{6,7},{15,8},{8,9},{9,10... | collective-permute-start | bytes 1179656 | tf_op jit(solution)/shard_map/while/body/eval_jaxpr/ppermute | solution.py:26
  524.6 25.6 %collective-permute-start.2 = (bf16[384,2,128]{2,0,1:T(8,128)(2,1)}, bf16[384,2,128]{2,0,1:T(8,128)(2,1)}, u32[]{:S(2)}, u32[]{:S(2)}) collective-permute-start(bf16[384,2,128]{2,0,1:T(8,128)(2,1)} %copy.225), channel_id=1, source_target_pairs={{7,0},{0,1},{1,2},{2,3},{3,4},{4,5},{5,6},{6,7},{15,8},{8,9},{9,10... | collective-permute-start | bytes 589832 | tf_op jit(solution)/shard_map/while/body/eval_jaxpr/ppermute | solution.py:26
  525.5 27.4 %collective-permute-start.3 = (bf16[384,2,128]{2,0,1:T(8,128)(2,1)}, bf16[384,2,128]{2,0,1:T(8,128)(2,1)}, u32[]{:S(2)}, u32[]{:S(2)}) collective-permute-start(bf16[384,2,128]{2,0,1:T(8,128)(2,1)} %copy.226), channel_id=1, source_target_pairs={{7,0},{0,1},{1,2},{2,3},{3,4},{4,5},{5,6},{6,7},{15,8},{8,9},{9,10... | collective-permute-start | bytes 589832 | tf_op jit(solution)/shard_map/while/body/eval_jaxpr/ppermute | solution.py:26
  562.3 28.8 %collective-permute-start.4 = (f32[384,2,128]{2,0,1:T(8,128)}, f32[384,2,128]{2,0,1:T(8,128)}, u32[]{:S(2)}, u32[]{:S(2)}) collective-permute-start(f32[384,2,128]{2,0,1:T(8,128)} %fusion.268), channel_id=1, source_target_pairs={{7,0},{0,1},{1,2},{2,3},{3,4},{4,5},{5,6},{6,7},{15,8},{8,9},{9,10... | collective-permute-start | bytes 1179656 | tf_op jit(solution)/shard_map/while/body/eval_jaxpr/ppermute | solution.py:26
  564.5 26.7 %collective-permute-start.5 = (f32[384,2,128]{2,0,1:T(8,128)}, f32[384,2,128]{2,0,1:T(8,128)}, u32[]{:S(2)}, u32[]{:S(2)}) collective-permute-start(f32[384,2,128]{2,0,1:T(8,128)} %fusion.269), channel_id=1, source_target_pairs={{7,0},{0,1},{1,2},{2,3},{3,4},{4,5},{5,6},{6,7},{15,8},{8,9},{9,10... | collective-permute-start | bytes 1179656 | tf_op jit(solution)/shard_map/while/body/eval_jaxpr/ppermute | solution.py:26
  564.5 24.6 %collective-permute-start.2 = (bf16[384,2,128]{2,0,1:T(8,128)(2,1)}, bf16[384,2,128]{2,0,1:T(8,128)(2,1)}, u32[]{:S(2)}, u32[]{:S(2)}) collective-permute-start(bf16[384,2,128]{2,0,1:T(8,128)(2,1)} %copy.225), channel_id=1, source_target_pairs={{7,0},{0,1},{1,2},{2,3},{3,4},{4,5},{5,6},{6,7},{15,8},{8,9},{9,10... | collective-permute-start | bytes 589832 | tf_op jit(solution)/shard_map/while/body/eval_jaxpr/ppermute | solution.py:26
  564.5 26.7 %collective-permute-start.3 = (bf16[384,2,128]{2,0,1:T(8,128)(2,1)}, bf16[384,2,128]{2,0,1:T(8,128)(2,1)}, u32[]{:S(2)}, u32[]{:S(2)}) collective-permute-start(bf16[384,2,128]{2,0,1:T(8,128)(2,1)} %copy.226), channel_id=1, source_target_pairs={{7,0},{0,1},{1,2},{2,3},{3,4},{4,5},{5,6},{6,7},{15,8},{8,9},{9,10... | collective-permute-start | bytes 589832 | tf_op jit(solution)/shard_map/while/body/eval_jaxpr/ppermute | solution.py:26
  600.6 28.0 %collective-permute-start.4 = (f32[384,2,128]{2,0,1:T(8,128)}, f32[384,2,128]{2,0,1:T(8,128)}, u32[]{:S(2)}, u32[]{:S(2)}) collective-permute-start(f32[384,2,128]{2,0,1:T(8,128)} %fusion.268), channel_id=1, source_target_pairs={{7,0},{0,1},{1,2},{2,3},{3,4},{4,5},{5,6},{6,7},{15,8},{8,9},{9,10... | collective-permute-start | bytes 1179656 | tf_op jit(solution)/shard_map/while/body/eval_jaxpr/ppermute | solution.py:26
  602.8 25.9 %collective-permute-start.5 = (f32[384,2,128]{2,0,1:T(8,128)}, f32[384,2,128]{2,0,1:T(8,128)}, u32[]{:S(2)}, u32[]{:S(2)}) collective-permute-start(f32[384,2,128]{2,0,1:T(8,128)} %fusion.269), channel_id=1, source_target_pairs={{7,0},{0,1},{1,2},{2,3},{3,4},{4,5},{5,6},{6,7},{15,8},{8,9},{9,10... | collective-permute-start | bytes 1179656 | tf_op jit(solution)/shard_map/while/body/eval_jaxpr/ppermute | solution.py:26
  602.8 23.8 %collective-permute-start.2 = (bf16[384,2,128]{2,0,1:T(8,128)(2,1)}, bf16[384,2,128]{2,0,1:T(8,128)(2,1)}, u32[]{:S(2)}, u32[]{:S(2)}) collective-permute-start(bf16[384,2,128]{2,0,1:T(8,128)(2,1)} %copy.225), channel_id=1, source_target_pairs={{7,0},{0,1},{1,2},{2,3},{3,4},{4,5},{5,6},{6,7},{15,8},{8,9},{9,10... | collective-permute-start | bytes 589832 | tf_op jit(solution)/shard_map/while/body/eval_jaxpr/ppermute | solution.py:26
  602.8 25.9 %collective-permute-start.3 = (bf16[384,2,128]{2,0,1:T(8,128)(2,1)}, bf16[384,2,128]{2,0,1:T(8,128)(2,1)}, u32[]{:S(2)}, u32[]{:S(2)}) collective-permute-start(bf16[384,2,128]{2,0,1:T(8,128)(2,1)} %copy.226), channel_id=1, source_target_pairs={{7,0},{0,1},{1,2},{2,3},{3,4},{4,5},{5,6},{6,7},{15,8},{8,9},{9,10... | collective-permute-start | bytes 589832 | tf_op jit(solution)/shard_map/while/body/eval_jaxpr/ppermute | solution.py:26
  638.1 27.1 %collective-permute-start.4 = (f32[384,2,128]{2,0,1:T(8,128)}, f32[384,2,128]{2,0,1:T(8,128)}, u32[]{:S(2)}, u32[]{:S(2)}) collective-permute-start(f32[384,2,128]{2,0,1:T(8,128)} %fusion.268), channel_id=1, source_target_pairs={{7,0},{0,1},{1,2},{2,3},{3,4},{4,5},{5,6},{6,7},{15,8},{8,9},{9,10... | collective-permute-start | bytes 1179656 | tf_op jit(solution)/shard_map/while/body/eval_jaxpr/ppermute | solution.py:26
  640.2 25.0 %collective-permute-start.5 = (f32[384,2,128]{2,0,1:T(8,128)}, f32[384,2,128]{2,0,1:T(8,128)}, u32[]{:S(2)}, u32[]{:S(2)}) collective-permute-start(f32[384,2,128]{2,0,1:T(8,128)} %fusion.269), channel_id=1, source_target_pairs={{7,0},{0,1},{1,2},{2,3},{3,4},{4,5},{5,6},{6,7},{15,8},{8,9},{9,10... | collective-permute-start | bytes 1179656 | tf_op jit(solution)/shard_map/while/body/eval_jaxpr/ppermute | solution.py:26
  640.2 22.9 %collective-permute-start.2 = (bf16[384,2,128]{2,0,1:T(8,128)(2,1)}, bf16[384,2,128]{2,0,1:T(8,128)(2,1)}, u32[]{:S(2)}, u32[]{:S(2)}) collective-permute-start(bf16[384,2,128]{2,0,1:T(8,128)(2,1)} %copy.225), channel_id=1, source_target_pairs={{7,0},{0,1},{1,2},{2,3},{3,4},{4,5},{5,6},{6,7},{15,8},{8,9},{9,10... | collective-permute-start | bytes 589832 | tf_op jit(solution)/shard_map/while/body/eval_jaxpr/ppermute | solution.py:26
  640.2 25.0 %collective-permute-start.3 = (bf16[384,2,128]{2,0,1:T(8,128)(2,1)}, bf16[384,2,128]{2,0,1:T(8,128)(2,1)}, u32[]{:S(2)}, u32[]{:S(2)}) collective-permute-start(bf16[384,2,128]{2,0,1:T(8,128)(2,1)} %copy.226), channel_id=1, source_target_pairs={{7,0},{0,1},{1,2},{2,3},{3,4},{4,5},{5,6},{6,7},{15,8},{8,9},{9,10... | collective-permute-start | bytes 589832 | tf_op jit(solution)/shard_map/while/body/eval_jaxpr/ppermute | solution.py:26
  674.7 26.3 %collective-permute-start.4 = (f32[384,2,128]{2,0,1:T(8,128)}, f32[384,2,128]{2,0,1:T(8,128)}, u32[]{:S(2)}, u32[]{:S(2)}) collective-permute-start(f32[384,2,128]{2,0,1:T(8,128)} %fusion.268), channel_id=1, source_target_pairs={{7,0},{0,1},{1,2},{2,3},{3,4},{4,5},{5,6},{6,7},{15,8},{8,9},{9,10... | collective-permute-start | bytes 1179656 | tf_op jit(solution)/shard_map/while/body/eval_jaxpr/ppermute | solution.py:26
  676.8 24.2 %collective-permute-start.5 = (f32[384,2,128]{2,0,1:T(8,128)}, f32[384,2,128]{2,0,1:T(8,128)}, u32[]{:S(2)}, u32[]{:S(2)}) collective-permute-start(f32[384,2,128]{2,0,1:T(8,128)} %fusion.269), channel_id=1, source_target_pairs={{7,0},{0,1},{1,2},{2,3},{3,4},{4,5},{5,6},{6,7},{15,8},{8,9},{9,10... | collective-permute-start | bytes 1179656 | tf_op jit(solution)/shard_map/while/body/eval_jaxpr/ppermute | solution.py:26
  676.8 22.0 %collective-permute-start.2 = (bf16[384,2,128]{2,0,1:T(8,128)(2,1)}, bf16[384,2,128]{2,0,1:T(8,128)(2,1)}, u32[]{:S(2)}, u32[]{:S(2)}) collective-permute-start(bf16[384,2,128]{2,0,1:T(8,128)(2,1)} %copy.225), channel_id=1, source_target_pairs={{7,0},{0,1},{1,2},{2,3},{3,4},{4,5},{5,6},{6,7},{15,8},{8,9},{9,10... | collective-permute-start | bytes 589832 | tf_op jit(solution)/shard_map/while/body/eval_jaxpr/ppermute | solution.py:26
  676.8 24.1 %collective-permute-start.3 = (bf16[384,2,128]{2,0,1:T(8,128)(2,1)}, bf16[384,2,128]{2,0,1:T(8,128)(2,1)}, u32[]{:S(2)}, u32[]{:S(2)}) collective-permute-start(bf16[384,2,128]{2,0,1:T(8,128)(2,1)} %copy.226), channel_id=1, source_target_pairs={{7,0},{0,1},{1,2},{2,3},{3,4},{4,5},{5,6},{6,7},{15,8},{8,9},{9,10... | collective-permute-start | bytes 589832 | tf_op jit(solution)/shard_map/while/body/eval_jaxpr/ppermute | solution.py:26
  710.7 8.5 %collective-permute-start.7 = (bf16[384,2,128]{0,2,1:T(8,128)(2,1)}, bf16[384,2,128]{0,2,1:T(8,128)(2,1)}, u32[]{:S(2)}, u32[]{:S(2)}) collective-permute-start(bf16[384,2,128]{0,2,1:T(8,128)(2,1)} %fusion.171), channel_id=1, source_target_pairs={{7,0},{0,1},{1,2},{2,3},{3,4},{4,5},{5,6},{6,7},{15,8},{8,9},{9,10... | collective-permute-start | bytes 589832 | tf_op jit(solution)/shard_map/ppermute | solution.py:26
  714.9 8.1 %collective-permute-start.6 = (bf16[384,2,128]{2,0,1:T(8,128)(2,1)}, bf16[384,2,128]{2,0,1:T(8,128)(2,1)}, u32[]{:S(2)}, u32[]{:S(2)}) collective-permute-start(bf16[384,2,128]{2,0,1:T(8,128)(2,1)} %fusion.170), channel_id=1, source_target_pairs={{7,0},{0,1},{1,2},{2,3},{3,4},{4,5},{5,6},{6,7},{15,8},{8,9},{9,10... | collective-permute-start | bytes 589832 | tf_op jit(solution)/shard_map/ppermute | solution.py:26
  (85 other events, 2777.5 us)
Sparse Core Ops, SparseCore 0:
  179.0 121.1 reduce-scatter.6
  303.0 76.6 all-gather.1
  421.6 137.0 reduce-scatter.4
